TPU v7x, 32 devices: a whole 2x2x4 slice. The times are simulated.
32 devices in a mesh: box: 8 (over z, y), dir: 4 (over x, core).
Axes of the slice: x: 2, y: 2, z: 4, core: 2. Of those that a mesh axis runs over, the one named last changes fastest.
Arguments:
- child_pattern: float32 [1024, 4, 128, 128], P('box', None, 'dir'), may hold values from -5 to 5
- octant: int32 [1024], P('box'), may hold values from 0 to 7, as said below
- shift_angle: float32 [8, 256, 256], replicated, may hold values from -3.140625 to 3.140625
- trans_table: bfloat16 [316, 2, 256, 256], P(None, None, 'dir'), may hold values from -2 to 2
- pair_near: int32 [1536], P('box'), may hold values from 0 to 15, as said below
- pair_far: int32 [1536], P('box'), may hold values from 0 to 47, as said below
- pair_class: int32 [1536], P('box'), may hold values from 0 to 315
- pair_live: int32 [1536], P('box'), may hold values from 0 to 1, as said below
Outputs:
- aggregated: float32 [128, 4, 256, 256], P('box', None, 'dir')
- incoming: float32 [128, 4, 256, 256], P('box', None, 'dir')
Inputs may be any that keep to these rules, and one draw needn't show every extreme that they name: `octant`: within each parent's eight consecutive children, a permutation of 0 to 7. `pair_near`: index of the pair's first box among the 16 boxes of the device that holds the slot. `pair_far`: index into the boxes of the slot's own device followed by those of the next 2 devices along box; never the pair's first box, never past the last box. `pair_live`: each device's live slots come first; some device has all 192 slots live.
All inputs are finite; a program needn't handle non-finite values.
Results may differ from a plain program's by a relative error of at most 0.0003.
Values sent between devices are 32-bit elements; how exact they have to be, the bound alone decides.
No kernel may reach another device: no remote copies, remote signals or barrier semaphores. Data moves between devices by JAX's collectives and lax.ppermute only.
A program may use at most 384 MiB of HBM per device.

v0:
```python
import functools
import math

import jax
import jax.numpy as jnp
from jax import lax
from jax.experimental import pallas as pl
from jax.experimental.pallas import tpu as pltpu
from jax.sharding import PartitionSpec as P

REACH = 2
THETA1 = 128
PHI1 = 128
THETA2 = 256
PHI2 = 256
ROWS = 16
TABLE_PIECES = 4


HIGHEST = lax.Precision.HIGHEST


def passed_along(value, axis, steps):
    count = lax.axis_size(axis)
    first, last = (max(0, -steps), min(count, count - steps))
    return lax.ppermute(value, axis, [(source, source + steps) for source in range(first, last)])


def interp_rows(size_in, size_out, count):
    target_pos = jnp.arange(count, dtype=jnp.int32)
    source_pos = jnp.arange(size_in, dtype=jnp.int32)
    offset = target_pos[:, None] - 2 * source_pos[None, :]
    is_odd = offset % 2 == 1
    safe_off = jnp.where(is_odd, offset, 1).astype(jnp.float32)
    kernel = jnp.sin(math.pi * safe_off / 2.0) / (size_in * jnp.tan(math.pi * safe_off / size_out))
    inner = jnp.where(is_odd, kernel, jnp.zeros_like(kernel))
    return jnp.where(offset == 0, jnp.ones_like(kernel), inner)


def interpolate(fields, theta_map, phi_map):
    widened = jnp.einsum("...t,ut->...u", fields, theta_map, precision=lax.Precision.HIGH)
    return jnp.einsum("qp,...pu->...qu", phi_map, widened, precision=lax.Precision.HIGH)


def select_rows(indices, table):
    count = table.shape[0]
    flat_ids = indices.reshape(-1)
    row_ids = jnp.arange(count, dtype=jnp.int32)
    onehot = (flat_ids[:, None] == row_ids[None, :]).astype(table.dtype)
    flat_table = table.reshape(count, -1)
    picked = jnp.dot(onehot, flat_table, precision=HIGHEST, preferred_element_type=jnp.float32)
    return picked.reshape(indices.shape + table.shape[1:])


def shift_sum(fields, cos_table, sin_table):
    groups = fields.shape[0]
    cosine = cos_table[None, :, None]
    sine = sin_table[None, :, None]
    shaped = fields.reshape(groups, 8, 2, 2, fields.shape[3], fields.shape[4])
    real_part = shaped[:, :, :, 0]
    imag_part = shaped[:, :, :, 1]
    new_real = jnp.sum(cosine * real_part - sine * imag_part, axis=1)
    new_imag = jnp.sum(sine * real_part + cosine * imag_part, axis=1)
    return jnp.stack([new_real, new_imag], axis=2).reshape(
        groups, 4, fields.shape[3], fields.shape[4]
    )


def pair_kernel(offsets, has_init, tgt_ref, src_ref, cls_ref, order_ref, span_ref, table_hbm, *rest):
    blocks = rest[: len(offsets)]
    out_hbm, table, sources, acc, sems, out_sem = rest[-6:]
    agg_hbm = None if has_init else rest[-7]
    if agg_hbm is not None:
        out_hbm, agg_hbm = agg_hbm, out_hbm
    rows = table.shape[2]
    classes = table.shape[0]
    pieces = [(p * classes // TABLE_PIECES, (p + 1) * classes // TABLE_PIECES) for p in range(TABLE_PIECES)]
    copies = [
        pltpu.make_async_copy(table_hbm.at[pl.ds(a, b - a)], table.at[pl.ds(a, b - a)], sems.at[p])
        for p, (a, b) in enumerate(pieces)
    ]
    for b, (block, first) in enumerate(zip(blocks, offsets)):
        copies.append(
            pltpu.make_async_copy(
                block, sources.at[pl.ds(first, block.shape[0])], sems.at[TABLE_PIECES + b]
            )
        )
    if has_init:
        copies.append(
            pltpu.make_async_copy(rest[len(offsets)], acc, sems.at[TABLE_PIECES + len(blocks)])
        )
    for c in copies:
        c.start()
    if not has_init:
        acc[...] = jnp.zeros_like(acc)
    for c in copies:
        c.wait()

    def item(i, carry):
        if True:
            j = order_ref[i]
            t = tgt_ref[j]
            s = src_ref[j]
            k = cls_ref[j]

            def chunk(j, inner):
                r0 = pl.multiple_of(j * ROWS, ROWS)
                win = pl.ds(r0, ROWS)
                tr = table[k, 0, win, :].astype(jnp.float32)
                ti = table[k, 1, win, :].astype(jnp.float32)
                for q in range(2):
                    pr = sources[s, 2 * q, win, :]
                    pi = sources[s, 2 * q + 1, win, :]
                    acc[t, 2 * q, win, :] += tr * pr - ti * pi
                    acc[t, 2 * q + 1, win, :] += ti * pr + tr * pi
                return inner

            lax.fori_loop(0, rows // ROWS, chunk, 0, unroll=True)

        return carry

    if agg_hbm is not None:
        local = pltpu.make_async_copy(sources.at[pl.ds(0, acc.shape[0])], agg_hbm, out_sem.at[1])
        local.start()
    lax.fori_loop(span_ref[0], span_ref[1], item, 0)
    done = pltpu.make_async_copy(acc, out_hbm, out_sem.at[0])
    done.start()
    done.wait()
    if agg_hbm is not None:
        local.wait()


def translate_pairs(items, trans_table, blocks, offsets, box_dev, init=None):
    tgt, src, cls, order, span = items
    shape = (box_dev,) + blocks[0].shape[1:]
    smem = pl.BlockSpec(memory_space=pltpu.SMEM)
    anywhere = pl.BlockSpec(memory_space=pl.ANY)
    extra = [] if init is None else [init]
    size = math.prod(shape)
    cost = pl.CostEstimate(
        flops=8 * size * tgt.shape[0] // 4,
        transcendentals=0,
        bytes_accessed=trans_table.size * 2 + 4 * size * (len(blocks) + 2),
    )
    return pl.pallas_call(
        functools.partial(pair_kernel, tuple(offsets), init is not None),
        out_shape=[jax.ShapeDtypeStruct(shape, jnp.float32)] * (1 if init is not None else 2),
        in_specs=[smem] * 5 + [anywhere] * (1 + len(blocks) + len(extra)),
        out_specs=[anywhere] * (1 if init is not None else 2),
        scratch_shapes=[
            pltpu.VMEM(trans_table.shape, trans_table.dtype),
            pltpu.VMEM(((2 * REACH + 1) * box_dev,) + shape[1:], jnp.float32),
            pltpu.VMEM(shape, jnp.float32),
            pltpu.SemaphoreType.DMA((TABLE_PIECES + 1 + len(blocks),)),
            pltpu.SemaphoreType.DMA((2,)),
        ],
        input_output_aliases={} if init is None else {6 + len(blocks): 0},
        cost_estimate=cost,
        compiler_params=pltpu.CompilerParams(vmem_limit_bytes=66_000_000),
    )(tgt, src, cls, order, span, trans_table, *blocks, *extra)


def pair_lists(pair_near, pair_far, pair_class, pair_live):
    packed = jnp.stack([pair_near, pair_far, pair_class, pair_live])
    return [packed] + [passed_along(packed, "box", o) for o in range(1, REACH + 1)]


def pair_items(lists, pair_near, pair_far, pair_class, pair_live, box_dev, classes):
    tgt = [pair_near]
    src = [pair_far]
    cls = [pair_class]
    live = [pair_live]
    for o, lst in enumerate(lists):
        near, far, k, alive = lst[0], lst[1], lst[2], lst[3]
        tgt.append(far - o * box_dev)
        base = 0 if o == 0 else (REACH + o) * box_dev
        src.append(near + base)
        cls.append((k + classes // 2) % classes)
        live.append(jnp.where(far // box_dev == o, alive, 0))
    return [jnp.concatenate(x).astype(jnp.int32) for x in (tgt, src, cls, live)]


def body(
    child_pattern, octant, shift_angle, trans_table, pair_near, pair_far, pair_class, pair_live
):
    dir_count = lax.axis_size("dir")
    dir_index = lax.axis_index("dir")
    box_dev = child_pattern.shape[0] // 8
    classes = trans_table.shape[0]
    lists = pair_lists(pair_near, pair_far, pair_class, pair_live)
    theta_map = interp_rows(THETA1, THETA2, THETA2)
    phi_map = interp_rows(PHI1, PHI2, PHI2)
    cos_table = jnp.cos(shift_angle)
    sin_table = jnp.sin(shift_angle)
    grouped = child_pattern.reshape(box_dev, 8, 4, PHI1 // dir_count, THETA1)
    octants = octant.reshape(box_dev, 8)
    slots = jnp.arange(8, dtype=jnp.int32)
    by_octant = jnp.sum(
        jnp.where(octants[:, :, None] == slots[None, None, :], slots[None, :, None], 0), axis=1
    )
    chunks = 1
    while chunks < 4 and box_dev % (2 * chunks * dir_count) == 0:
        chunks *= 2
    per_chunk = box_dev // chunks
    per_dev = per_chunk // dir_count
    parts = []
    blocks = []
    offsets = []

    def send(c, part):
        moved = [part]
        moved += [passed_along(part, "box", -o) for o in range(1, REACH + 1)]
        moved += [passed_along(part, "box", o) for o in range(1, REACH + 1)]
        for b, block in enumerate(moved):
            blocks.append(block)
            offsets.append(b * box_dev + c * per_chunk)

    for c in range(chunks):
        piece = jnp.take_along_axis(
            grouped[c * per_chunk : (c + 1) * per_chunk],
            by_octant[c * per_chunk : (c + 1) * per_chunk, :, None, None, None],
            axis=1,
        )
        gathered = lax.all_to_all(piece, "dir", split_axis=0, concat_axis=3, tiled=True)
        if c >= 2:
            lo = (c - 2) * (2 * REACH + 1) + 1
            hi = (c - 1) * (2 * REACH + 1)
            sent, gathered = lax.optimization_barrier((blocks[lo:hi], gathered))
            blocks[lo:hi] = sent
        if parts:
            parts[-1], gathered = lax.optimization_barrier((parts[-1], gathered))
            send(c - 1, parts[-1])
        else:
            lists, gathered = lax.optimization_barrier((lists, gathered))
        full_dirs = interpolate(gathered, theta_map, phi_map)
        summed = shift_sum(full_dirs, cos_table, sin_table)
        parts.append(lax.all_to_all(summed, "dir", split_axis=2, concat_axis=0, tiled=True))
    send(chunks - 1, parts[-1])
    items = pair_items(lists, pair_near, pair_far, pair_class, pair_live, box_dev, classes)
    tgt, src, cls, live = items
    late = (src >= box_dev) & (src % box_dev >= (chunks - 1) * per_chunk)
    key = jnp.where(live != 0, late.astype(jnp.int32), 2)
    order = jnp.argsort(key, stable=True).astype(jnp.int32)
    n_early = jnp.sum(key == 0).astype(jnp.int32)
    n_live = n_early + jnp.sum(key == 1).astype(jnp.int32)
    early_items = (tgt, src, cls, order, jnp.stack([jnp.int32(0), n_early]))
    late_items = (tgt, src, cls, order, jnp.stack([n_early, n_live]))
    cut = len(blocks) - 2 * REACH
    partial, aggregated = translate_pairs(
        early_items, trans_table, blocks[:cut], offsets[:cut], box_dev
    )
    (incoming,) = translate_pairs(
        late_items, trans_table, blocks[cut:], offsets[cut:], box_dev, init=partial
    )
    return (aggregated, incoming)


def solution(mesh):
    placed = (
        P("box", None, "dir", None),
        P("box"),
        P(),
        P(None, None, "dir", None),
        P("box"),
        P("box"),
        P("box"),
        P("box"),
    )
    return jax.shard_map(
        body,
        mesh=mesh,
        in_specs=placed,
        out_specs=(P("box", None, "dir", None), P("box", None, "dir", None)),
        check_vma=False,
    )
```

profile of v0, /device:TPU:22, one launch (start us, length us, event | category | flops | bytes accessed | tf_op | source)
XLA Modules:
  0.0 322.4 jit_solution(1239221039357761876)
XLA Ops:
  1.7 7.7 %fusion.93 = (f32[32,4,32,128]{3,2,1,0:T(8,128)}, f32[32,4,32,128]{3,2,1,0:T(8,128)}, f32[32,4,32,128]{3,2,1,0:T(8,128)}, f32[32,4,32,128]{3,2,1,0:T(8,128)}) fusion(f32[128,4,32,128]{3,2,1,0:T(8,128)} %param.10), kind=kLoop, calls=%fused_computation.184 | loop fusion | bytes 16777216 | tf_op jit(solution)/shard_map/slice | solution.py:220
  13.2 5.1 %all-to-all-start = ((f32[4,8,4,32,128]{4,3,2,1,0:T(8,128)}), f32[4,8,4,32,128]{4,3,2,1,0:T(8,128)}, u32[]{:S(2)}, u32[]{:S(2)}) async-start(f32[4,8,4,32,128]{4,3,2,1,0:T(8,128)} %broadcast_select_fusion.3), calls=%async_computation | async-start | bytes 4194304 | tf_op jit(solution)/shard_map/all_to_all | solution.py:224
  18.3 3.4 %collective-permute-start = (s32[4,192]{1,0:T(4,128)S(1)}, s32[4,192]{1,0:T(4,128)S(1)}, u32[]{:S(2)}, u32[]{:S(2)}) collective-permute-start(s32[4,192]{1,0:T(4,128)S(1)} %pad_add_fusion), channel_id=1, source_target_pairs={{0,4},{4,8},{8,12},{12,16},{16,20},{20,24},{24,28},{1,5},{5,9},{9,... | collective-permute-start | bytes 9224 | tf_op jit(solution)/shard_map/ppermute | solution.py:26
  28.5 8.2 %fusion.94 = (f32[8,256,256]{2,1,0:T(8,128)}, f32[8,256,256]{2,1,0:T(8,128)}) fusion(f32[8,256,256]{2,1,0:T(8,128)S(1)} %copy-done.11), kind=kLoop, calls=%fused_computation.185 | loop fusion | bytes 6291456 | tf_op jit(solution)/shard_map/cos | solution.py:193
  42.4 6.3 %all-to-all-start.2 = ((f32[4,8,4,32,128]{4,3,2,1,0:T(8,128)}), f32[4,8,4,32,128]{4,3,2,1,0:T(8,128)}, u32[]{:S(2)}, u32[]{:S(2)}) async-start(f32[4,8,4,32,128]{4,3,2,1,0:T(8,128)} %broadcast_select_fusion.2), calls=%async_computation.2 | async-start | bytes 4194304 | tf_op jit(solution)/shard_map/all_to_all | solution.py:224
  53.3 4.4 %fusion.19 = f32[8,4,256,256]{3,2,1,0:T(8,128)S(1)} fusion(f32[8,4,128,256]{2,3,1,0:T(8,128)S(1)} %fusion.6, s32[128]{0:T(128)S(1)} %iota_multiply_fusion), kind=kOutput, calls=%fused_computation.54 | convolution fusion | flops 1611333632 | bytes 12583424 | tf_op jit(solution)/shard_map/qp,...pu->...qu/dot_general | solution.py:42
  63.7 9.1 %all-to-all-done.2 = f32[4,8,4,32,128]{4,3,2,1,0:T(8,128)} async-done(((f32[4,8,4,32,128]{4,3,2,1,0:T(8,128)}), f32[4,8,4,32,128]{4,3,2,1,0:T(8,128)}, u32[]{:S(2)}, u32[]{:S(2)}) %all-to-all-start.2) | async-done | bytes 2097184 | tf_op jit(solution)/shard_map/all_to_all | solution.py:224
  72.8 5.2 %all-to-all-start.1 = ((f32[1,4,256,256]{3,1,0,2:T(4,128)}), f32[1,4,256,256]{3,1,0,2:T(4,128)S(1)}, u32[]{:S(2)}, u32[]{:S(2)}) async-start(f32[1,4,256,256]{3,1,0,2:T(4,128)} %copy.101), calls=%async_computation.1 | async-start | bytes 2097152 | tf_op jit(solution)/shard_map/all_to_all | solution.py:237
  78.1 3.6 %gather_fusion.2 = f32[32,4,32,128]{3,2,1,0:T(8,128)} fusion(f32[4,8,4,32,128]{4,3,2,1,0:T(8,128)} %bitcast.258, s32[32]{0:T(128)S(1)} %reshape.417), kind=kCustom, calls=%fused_computation.2.clone | custom fusion | bytes 4194560 | tf_op jit(solution)/shard_map/jit(take_along_axis)/gather | solution.py:219
  84.9 3.2 copy.105
  91.7 6.1 %all-to-all-start.3 = ((f32[4,8,4,32,128]{4,3,2,1,0:T(8,128)}), f32[4,8,4,32,128]{4,3,2,1,0:T(8,128)}, u32[]{:S(2)}, u32[]{:S(2)}) async-start(f32[4,8,4,32,128]{4,3,2,1,0:T(8,128)} %broadcast_select_fusion.1), calls=%async_computation.3 | async-start | bytes 4194304 | tf_op jit(solution)/shard_map/all_to_all | solution.py:224
  104.2 5.4 %collective-permute-start.4 = (f32[4,4,64,256]{3,2,1,0:T(8,128)S(1)}, f32[4,4,64,256]{3,2,1,0:T(8,128)}, u32[]{:S(2)}, u32[]{:S(2)}) collective-permute-start(f32[4,4,64,256]{3,2,1,0:T(8,128)S(1)} %bitcast.263), channel_id=1, source_target_pairs={{0,4},{4,8},{8,12},{12,16},{16,20},{20,24},{24,28},{1,5},{5,9},{9,... | collective-permute-start | bytes 3145736 | tf_op jit(solution)/shard_map/ppermute | solution.py:26
  114.5 4.4 %fusion.16 = f32[8,4,256,256]{3,2,1,0:T(8,128)S(1)} fusion(f32[8,4,128,256]{2,3,1,0:T(8,128)S(1)} %fusion.4, s32[128]{0:T(128)S(1)} %iota_multiply_fusion), kind=kOutput, calls=%fused_computation.51 | convolution fusion | flops 1611333632 | bytes 12583424 | tf_op jit(solution)/shard_map/qp,...pu->...qu/dot_general | solution.py:42
  127.2 4.2 %all-to-all-start.4 = ((f32[1,4,256,256]{3,1,0,2:T(4,128)}), f32[1,4,256,256]{3,1,0,2:T(4,128)}, u32[]{:S(2)}, u32[]{:S(2)}) async-start(f32[1,4,256,256]{3,1,0,2:T(4,128)} %copy.112), calls=%async_computation.4 | async-start | bytes 2097152 | tf_op jit(solution)/shard_map/all_to_all | solution.py:237
  131.6 3.6 %gather_fusion.3 = f32[32,4,32,128]{3,2,1,0:T(8,128)} fusion(f32[4,8,4,32,128]{4,3,2,1,0:T(8,128)} %bitcast.257, s32[32]{0:T(128)S(1)} %reshape.422), kind=kCustom, calls=%fused_computation.3.clone | custom fusion | bytes 4194560 | tf_op jit(solution)/shard_map/jit(take_along_axis)/gather | solution.py:219
  138.3 3.2 copy.107
  144.3 6.1 %all-to-all-start.5 = ((f32[4,8,4,32,128]{4,3,2,1,0:T(8,128)}), f32[4,8,4,32,128]{4,3,2,1,0:T(8,128)}, u32[]{:S(2)}, u32[]{:S(2)}) async-start(f32[4,8,4,32,128]{4,3,2,1,0:T(8,128)} %broadcast_select_fusion), calls=%async_computation.5 | async-start | bytes 4194304 | tf_op jit(solution)/shard_map/all_to_all | solution.py:224
  158.8 5.8 %collective-permute-start.8 = (f32[4,4,64,256]{3,2,1,0:T(8,128)}, f32[4,4,64,256]{3,2,1,0:T(8,128)}, u32[]{:S(2)}, u32[]{:S(2)}) collective-permute-start(f32[4,4,64,256]{3,2,1,0:T(8,128)} %bitcast.243.rest_5_), channel_id=1, source_target_pairs={{0,4},{4,8},{8,12},{12,16},{16,20},{20,24},{24,28},{1,5},{5,9},{9,... | collective-permute-start | bytes 3145736 | tf_op jit(solution)/shard_map/ppermute | solution.py:26
  169.8 4.4 %fusion.13 = f32[8,4,256,256]{3,2,1,0:T(8,128)S(1)} fusion(f32[8,4,128,256]{2,3,1,0:T(8,128)S(1)} %fusion.2, s32[128]{0:T(128)S(1)} %iota_multiply_fusion), kind=kOutput, calls=%fused_computation.48 | convolution fusion | flops 1611333632 | bytes 12583424 | tf_op jit(solution)/shard_map/qp,...pu->...qu/dot_general | solution.py:42
  180.1 3.5 %all-to-all-start.6 = ((f32[1,4,256,256]{3,1,0,2:T(4,128)}), f32[1,4,256,256]{3,1,0,2:T(4,128)S(1)}, u32[]{:S(2)}, u32[]{:S(2)}) async-start(f32[1,4,256,256]{3,1,0,2:T(4,128)} %copy.121), calls=%async_computation.6 | async-start | bytes 2097152 | tf_op jit(solution)/shard_map/all_to_all | solution.py:237
  186.9 9.6 %all-to-all-done.6 = f32[1,4,256,256]{3,1,0,2:T(4,128)S(1)} async-done(((f32[1,4,256,256]{3,1,0,2:T(4,128)}), f32[1,4,256,256]{3,1,0,2:T(4,128)S(1)}, u32[]{:S(2)}, u32[]{:S(2)}) %all-to-all-start.6) | async-done | bytes 1048608 | tf_op jit(solution)/shard_map/all_to_all | solution.py:237
  203.7 5.8 %collective-permute-done.9.rest_9_ = f32[4,4,64,256]{3,2,1,0:T(8,128)} collective-permute-done((f32[4,4,64,256]{3,2,1,0:T(8,128)}, f32[4,4,64,256]{3,2,1,0:T(8,128)}, u32[]{:S(2)}, u32[]{:S(2)}) %collective-permute-start.9) | collective-permute-done | bytes 1048608 | tf_op jit(solution)/shard_map/ppermute | solution.py:26
  213.5 6.0 %collective-permute-start.12 = (f32[4,4,64,256]{3,2,1,0:T(8,128)S(1)}, f32[4,4,64,256]{3,2,1,0:T(8,128)}, u32[]{:S(2)}, u32[]{:S(2)}) collective-permute-start(f32[4,4,64,256]{3,2,1,0:T(8,128)S(1)} %bitcast.268), channel_id=1, source_target_pairs={{0,4},{4,8},{8,12},{12,16},{16,20},{20,24},{24,28},{1,5},{5,9},{9,... | collective-permute-start | bytes 3145736 | tf_op jit(solution)/shard_map/ppermute | solution.py:26
  222.3 4.4 %fusion.10 = f32[8,4,256,256]{3,2,1,0:T(8,128)S(1)} fusion(f32[8,4,128,256]{2,3,1,0:T(8,128)S(1)} %fusion, s32[128]{0:T(128)S(1)} %iota_multiply_fusion), kind=kOutput, calls=%fused_computation.45 | convolution fusion | flops 1611333632 | bytes 12583424 | tf_op jit(solution)/shard_map/qp,...pu->...qu/dot_general | solution.py:42
  230.5 3.8 %all-to-all-start.7 = ((f32[1,4,256,256]{3,1,0,2:T(4,128)}), f32[1,4,256,256]{3,1,0,2:T(4,128)S(1)}, u32[]{:S(2)}, u32[]{:S(2)}) async-start(f32[1,4,256,256]{3,1,0,2:T(4,128)} %copy.128), calls=%async_computation.7 | async-start | bytes 2097152 | tf_op jit(solution)/shard_map/all_to_all | solution.py:237
  240.2 4.4 %sort.17 = (s32[768]{0:T(1024)}, s32[768]{0:T(1024)}) sort(s32[768]{0:T(1024)S(1)} %get-tuple-element.59, s32[768]{0:T(1024)S(1)} %iota.36), dimensions={0}, to_apply=%region_1.3 | sort | flops 7680 | bytes 12288 | tf_op jit(solution)/shard_map/jit(argsort)/sort | solution.py:243
  250.2 7.4 %collective-permute-done.10.rest_11_ = f32[4,4,64,256]{3,2,1,0:T(8,128)} collective-permute-done((f32[4,4,64,256]{3,2,1,0:T(8,128)S(1)}, f32[4,4,64,256]{3,2,1,0:T(8,128)}, u32[]{:S(2)}, u32[]{:S(2)}) %collective-permute-start.10) | collective-permute-done | bytes 1048608 | tf_op jit(solution)/shard_map/ppermute | solution.py:26
  259.6 6.8 %collective-permute-start.16 = (f32[4,4,64,256]{3,2,1,0:T(8,128)}, f32[4,4,64,256]{3,2,1,0:T(8,128)}, u32[]{:S(2)}, u32[]{:S(2)}) collective-permute-start(f32[4,4,64,256]{3,2,1,0:T(8,128)} %bitcast.241.rest_15_), channel_id=1, source_target_pairs={{0,4},{4,8},{8,12},{12,16},{16,20},{20,24},{24,28},{1,5},{5,9},{9,... | collective-permute-start | bytes 3145736 | tf_op jit(solution)/shard_map/ppermute | solution.py:26
  270.6 26.0 %shard_map.95 = (f32[16,4,64,256]{3,2,1,0:T(8,128)}, f32[16,4,64,256]{3,2,1,0:T(8,128)}) custom-call(s32[768]{0:T(1024)} %pad_add_fusion.1.tgt_ref, s32[768]{0:T(1024)} %get-tuple-element.70.src_ref, s32[768]{0:T(1024)} %pad_add_fusion.3.cls_ref, s32[768]{0:T(1024)} %get-tuple-element.29.order_ref, s32[2]{0:T(128)} %pad_add_fusion.4.span_ref, ...), custom_call_target="tpu_custom_call" | custom-call | flops 1610612736 | bytes 96206848 | tf_op jit(solution)/shard_map/pallas_call | solution.py:145
  296.6 4.0 %collective-permute-done.14.rest_0_ = f32[4,4,64,256]{3,2,1,0:T(8,128)} collective-permute-done((f32[4,4,64,256]{3,2,1,0:T(8,128)}, f32[4,4,64,256]{3,2,1,0:T(8,128)}, u32[]{:S(2)}, u32[]{:S(2)}) %collective-permute-start.14) | collective-permute-done | bytes 1048608 | tf_op jit(solution)/shard_map/ppermute | solution.py:26
  303.7 4.3 %collective-permute-done.17.rest_3_ = f32[4,4,64,256]{3,2,1,0:T(8,128)} collective-permute-done((f32[4,4,64,256]{3,2,1,0:T(8,128)}, f32[4,4,64,256]{3,2,1,0:T(8,128)}, u32[]{:S(2)}, u32[]{:S(2)}) %collective-permute-start.17) | collective-permute-done | bytes 1048608 | tf_op jit(solution)/shard_map/ppermute | solution.py:26
  308.0 14.2 %shard_map.96 = f32[16,4,64,256]{3,2,1,0:T(8,128)} custom-call(s32[768]{0:T(1024)} %pad_add_fusion.1.tgt_ref, s32[768]{0:T(1024)} %get-tuple-element.70.src_ref, s32[768]{0:T(1024)} %pad_add_fusion.3.cls_ref, s32[768]{0:T(1024)} %get-tuple-element.29.order_ref, s32[2]{0:T(128)} %pad_add_fusion.5.span_ref, ...), custom_call_target="tpu_custom_call", output_to_operand_aliasing={{}: (10, {})} | custom-call | flops 1610612736 | bytes 45875200 | tf_op jit(solution)/shard_map/pallas_call | solution.py:145
  (137 shorter events, 120.4 us)
Async XLA Ops:
  13.2 5.1 %copy-start.16 = (s32[192]{0:T(256)S(1)}, s32[192]{0:T(256)}, u32[]{:S(2)}) copy-start(s32[192]{0:T(256)} %param.16) | copy-start | bytes 2308
  13.2 29.2 %all-to-all-start = ((f32[4,8,4,32,128]{4,3,2,1,0:T(8,128)}), f32[4,8,4,32,128]{4,3,2,1,0:T(8,128)}, u32[]{:S(2)}, u32[]{:S(2)}) async-start(f32[4,8,4,32,128]{4,3,2,1,0:T(8,128)} %broadcast_select_fusion.3), calls=%async_computation | async-start | bytes 4194304 | tf_op jit(solution)/shard_map/all_to_all | solution.py:224
  18.3 32.2 %collective-permute-start = (s32[4,192]{1,0:T(4,128)S(1)}, s32[4,192]{1,0:T(4,128)S(1)}, u32[]{:S(2)}, u32[]{:S(2)}) collective-permute-start(s32[4,192]{1,0:T(4,128)S(1)} %pad_add_fusion), channel_id=1, source_target_pairs={{0,4},{4,8},{8,12},{12,16},{16,20},{20,24},{24,28},{1,5},{5,9},{9,... | collective-permute-start | bytes 9224 | tf_op jit(solution)/shard_map/ppermute | solution.py:26
  21.7 28.8 %collective-permute-start.1 = (s32[4,192]{1,0:T(4,128)S(1)}, s32[4,192]{1,0:T(4,128)S(1)}, u32[]{:S(2)}, u32[]{:S(2)}) collective-permute-start(s32[4,192]{1,0:T(4,128)S(1)} %pad_add_fusion), channel_id=1, source_target_pairs={{0,8},{4,12},{8,16},{12,20},{16,24},{20,28},{1,9},{5,13},{9,17},{1... | collective-permute-start | bytes 9224 | tf_op jit(solution)/shard_map/ppermute | solution.py:26
  42.4 30.4 %all-to-all-start.2 = ((f32[4,8,4,32,128]{4,3,2,1,0:T(8,128)}), f32[4,8,4,32,128]{4,3,2,1,0:T(8,128)}, u32[]{:S(2)}, u32[]{:S(2)}) async-start(f32[4,8,4,32,128]{4,3,2,1,0:T(8,128)} %broadcast_select_fusion.2), calls=%async_computation.2 | async-start | bytes 4194304 | tf_op jit(solution)/shard_map/all_to_all | solution.py:224
  72.8 18.0 %all-to-all-start.1 = ((f32[1,4,256,256]{3,1,0,2:T(4,128)}), f32[1,4,256,256]{3,1,0,2:T(4,128)S(1)}, u32[]{:S(2)}, u32[]{:S(2)}) async-start(f32[1,4,256,256]{3,1,0,2:T(4,128)} %copy.101), calls=%async_computation.1 | async-start | bytes 2097152 | tf_op jit(solution)/shard_map/all_to_all | solution.py:237
  91.7 35.4 %all-to-all-start.3 = ((f32[4,8,4,32,128]{4,3,2,1,0:T(8,128)}), f32[4,8,4,32,128]{4,3,2,1,0:T(8,128)}, u32[]{:S(2)}, u32[]{:S(2)}) async-start(f32[4,8,4,32,128]{4,3,2,1,0:T(8,128)} %broadcast_select_fusion.1), calls=%async_computation.3 | async-start | bytes 4194304 | tf_op jit(solution)/shard_map/all_to_all | solution.py:224
  97.8 13.9 %copy-start.6 = (f32[1,8,4,4,32,128]{5,4,3,2,1,0:T(8,128)S(1)}, f32[1,8,4,4,32,128]{5,4,3,2,1,0:T(8,128)}, u32[]{:S(2)}) copy-start(f32[1,8,4,4,32,128]{5,4,3,2,1,0:T(8,128)} %copy.105) | copy-start | bytes 6291460
  99.4 15.1 %copy-start.7 = (f32[1,4,4,64,256]{4,3,1,2,0:T(8,128)}, f32[1,4,4,64,256]{4,3,1,2,0:T(8,128)S(1)}, u32[]{:S(2)}) copy-start(f32[1,4,4,64,256]{4,3,1,2,0:T(8,128)S(1)} %copy.159) | copy-start | bytes 3145732
  99.4 53.5 %collective-permute-start.2 = (f32[4,4,64,256]{3,2,1,0:T(8,128)S(1)}, f32[4,4,64,256]{3,2,1,0:T(8,128)}, u32[]{:S(2)}, u32[]{:S(2)}) collective-permute-start(f32[4,4,64,256]{3,2,1,0:T(8,128)S(1)} %bitcast.261), channel_id=1, source_target_pairs={{4,0},{8,4},{12,8},{16,12},{20,16},{24,20},{28,24},{5,1},{9,5},{13... | collective-permute-start | bytes 3145736 | tf_op jit(solution)/shard_map/ppermute | solution.py:26
  101.8 51.1 %collective-permute-start.3 = (f32[4,4,64,256]{3,2,1,0:T(8,128)S(1)}, f32[4,4,64,256]{3,2,1,0:T(8,128)}, u32[]{:S(2)}, u32[]{:S(2)}) collective-permute-start(f32[4,4,64,256]{3,2,1,0:T(8,128)S(1)} %bitcast.262), channel_id=1, source_target_pairs={{8,0},{12,4},{16,8},{20,12},{24,16},{28,20},{9,1},{13,5},{17,9},{2... | collective-permute-start | bytes 3145736 | tf_op jit(solution)/shard_map/ppermute | solution.py:26
  104.2 48.8 %collective-permute-start.4 = (f32[4,4,64,256]{3,2,1,0:T(8,128)S(1)}, f32[4,4,64,256]{3,2,1,0:T(8,128)}, u32[]{:S(2)}, u32[]{:S(2)}) collective-permute-start(f32[4,4,64,256]{3,2,1,0:T(8,128)S(1)} %bitcast.263), channel_id=1, source_target_pairs={{0,4},{4,8},{8,12},{12,16},{16,20},{20,24},{24,28},{1,5},{5,9},{9,... | collective-permute-start | bytes 3145736 | tf_op jit(solution)/shard_map/ppermute | solution.py:26
  109.5 44.7 %collective-permute-start.5 = (f32[4,4,64,256]{3,2,1,0:T(8,128)S(1)}, f32[4,4,64,256]{3,2,1,0:T(8,128)}, u32[]{:S(2)}, u32[]{:S(2)}) collective-permute-start(f32[4,4,64,256]{3,2,1,0:T(8,128)S(1)} %bitcast.264), channel_id=1, source_target_pairs={{0,8},{4,12},{8,16},{12,20},{16,24},{20,28},{1,9},{5,13},{9,17},{1... | collective-permute-start | bytes 3145736 | tf_op jit(solution)/shard_map/ppermute | solution.py:26
  127.2 17.2 %all-to-all-start.4 = ((f32[1,4,256,256]{3,1,0,2:T(4,128)}), f32[1,4,256,256]{3,1,0,2:T(4,128)}, u32[]{:S(2)}, u32[]{:S(2)}) async-start(f32[1,4,256,256]{3,1,0,2:T(4,128)} %copy.112), calls=%async_computation.4 | async-start | bytes 2097152 | tf_op jit(solution)/shard_map/all_to_all | solution.py:237
  144.3 35.8 %all-to-all-start.5 = ((f32[4,8,4,32,128]{4,3,2,1,0:T(8,128)}), f32[4,8,4,32,128]{4,3,2,1,0:T(8,128)}, u32[]{:S(2)}, u32[]{:S(2)}) async-start(f32[4,8,4,32,128]{4,3,2,1,0:T(8,128)} %broadcast_select_fusion), calls=%async_computation.5 | async-start | bytes 4194304 | tf_op jit(solution)/shard_map/all_to_all | solution.py:224
  150.4 16.6 %copy-start.5 = (f32[1,8,4,4,32,128]{5,4,3,2,1,0:T(8,128)S(1)}, f32[1,8,4,4,32,128]{5,4,3,2,1,0:T(8,128)}, u32[]{:S(2)}) copy-start(f32[1,8,4,4,32,128]{5,4,3,2,1,0:T(8,128)} %copy.107) | copy-start | bytes 6291460
  154.2 47.3 %collective-permute-start.6 = (f32[4,4,64,256]{3,2,1,0:T(8,128)}, f32[4,4,64,256]{3,2,1,0:T(8,128)}, u32[]{:S(2)}, u32[]{:S(2)}) collective-permute-start(f32[4,4,64,256]{3,2,1,0:T(8,128)} %bitcast.243.rest_5_), channel_id=1, source_target_pairs={{4,0},{8,4},{12,8},{16,12},{20,16},{24,20},{28,24},{5,1},{9,5},{13... | collective-permute-start | bytes 3145736 | tf_op jit(solution)/shard_map/ppermute | solution.py:26
  156.1 45.4 %collective-permute-start.7 = (f32[4,4,64,256]{3,2,1,0:T(8,128)}, f32[4,4,64,256]{3,2,1,0:T(8,128)}, u32[]{:S(2)}, u32[]{:S(2)}) collective-permute-start(f32[4,4,64,256]{3,2,1,0:T(8,128)} %bitcast.243.rest_5_), channel_id=1, source_target_pairs={{8,0},{12,4},{16,8},{20,12},{24,16},{28,20},{9,1},{13,5},{17,9},{2... | collective-permute-start | bytes 3145736 | tf_op jit(solution)/shard_map/ppermute | solution.py:26
  158.8 44.9 %collective-permute-start.8 = (f32[4,4,64,256]{3,2,1,0:T(8,128)}, f32[4,4,64,256]{3,2,1,0:T(8,128)}, u32[]{:S(2)}, u32[]{:S(2)}) collective-permute-start(f32[4,4,64,256]{3,2,1,0:T(8,128)} %bitcast.243.rest_5_), channel_id=1, source_target_pairs={{0,4},{4,8},{8,12},{12,16},{16,20},{20,24},{24,28},{1,5},{5,9},{9,... | collective-permute-start | bytes 3145736 | tf_op jit(solution)/shard_map/ppermute | solution.py:26
  164.6 45.0 %collective-permute-start.9 = (f32[4,4,64,256]{3,2,1,0:T(8,128)}, f32[4,4,64,256]{3,2,1,0:T(8,128)}, u32[]{:S(2)}, u32[]{:S(2)}) collective-permute-start(f32[4,4,64,256]{3,2,1,0:T(8,128)} %bitcast.243.rest_5_), channel_id=1, source_target_pairs={{0,8},{4,12},{8,16},{12,20},{16,24},{20,28},{1,9},{5,13},{9,17},{1... | collective-permute-start | bytes 3145736 | tf_op jit(solution)/shard_map/ppermute | solution.py:26
  180.1 16.3 %all-to-all-start.6 = ((f32[1,4,256,256]{3,1,0,2:T(4,128)}), f32[1,4,256,256]{3,1,0,2:T(4,128)S(1)}, u32[]{:S(2)}, u32[]{:S(2)}) async-start(f32[1,4,256,256]{3,1,0,2:T(4,128)} %copy.121), calls=%async_computation.6 | async-start | bytes 2097152 | tf_op jit(solution)/shard_map/all_to_all | solution.py:237
  197.5 22.1 %copy-start.4 = (f32[1,8,4,4,32,128]{5,4,3,2,1,0:T(8,128)S(1)}, f32[1,8,4,4,32,128]{5,4,3,2,1,0:T(8,128)}, u32[]{:S(2)}) copy-start(f32[1,8,4,4,32,128]{5,4,3,2,1,0:T(8,128)} %copy.116) | copy-start | bytes 6291460
  199.0 36.7 %copy-start.8 = (f32[1,4,4,64,256]{4,3,1,2,0:T(8,128)}, f32[1,4,4,64,256]{4,3,1,2,0:T(8,128)S(1)}, u32[]{:S(2)}) copy-start(f32[1,4,4,64,256]{4,3,1,2,0:T(8,128)S(1)} %copy.157) | copy-start | bytes 3145732
  209.6 48.0 %collective-permute-start.10 = (f32[4,4,64,256]{3,2,1,0:T(8,128)S(1)}, f32[4,4,64,256]{3,2,1,0:T(8,128)}, u32[]{:S(2)}, u32[]{:S(2)}) collective-permute-start(f32[4,4,64,256]{3,2,1,0:T(8,128)S(1)} %bitcast.266), channel_id=1, source_target_pairs={{4,0},{8,4},{12,8},{16,12},{20,16},{24,20},{28,24},{5,1},{9,5},{13... | collective-permute-start | bytes 3145736 | tf_op jit(solution)/shard_map/ppermute | solution.py:26
  211.5 48.1 %collective-permute-start.11 = (f32[4,4,64,256]{3,2,1,0:T(8,128)S(1)}, f32[4,4,64,256]{3,2,1,0:T(8,128)}, u32[]{:S(2)}, u32[]{:S(2)}) collective-permute-start(f32[4,4,64,256]{3,2,1,0:T(8,128)S(1)} %bitcast.267), channel_id=1, source_target_pairs={{8,0},{12,4},{16,8},{20,12},{24,16},{28,20},{9,1},{13,5},{17,9},{2... | collective-permute-start | bytes 3145736 | tf_op jit(solution)/shard_map/ppermute | solution.py:26
  213.5 52.8 %collective-permute-start.12 = (f32[4,4,64,256]{3,2,1,0:T(8,128)S(1)}, f32[4,4,64,256]{3,2,1,0:T(8,128)}, u32[]{:S(2)}, u32[]{:S(2)}) collective-permute-start(f32[4,4,64,256]{3,2,1,0:T(8,128)S(1)} %bitcast.268), channel_id=1, source_target_pairs={{0,4},{4,8},{8,12},{12,16},{16,20},{20,24},{24,28},{1,5},{5,9},{9,... | collective-permute-start | bytes 3145736 | tf_op jit(solution)/shard_map/ppermute | solution.py:26
  230.5 16.6 %all-to-all-start.7 = ((f32[1,4,256,256]{3,1,0,2:T(4,128)}), f32[1,4,256,256]{3,1,0,2:T(4,128)S(1)}, u32[]{:S(2)}, u32[]{:S(2)}) async-start(f32[1,4,256,256]{3,1,0,2:T(4,128)} %copy.128), calls=%async_computation.7 | async-start | bytes 2097152 | tf_op jit(solution)/shard_map/all_to_all | solution.py:237
  235.7 34.0 %collective-permute-start.13 = (f32[4,4,64,256]{3,2,1,0:T(8,128)S(1)}, f32[4,4,64,256]{3,2,1,0:T(8,128)S(1)}, u32[]{:S(2)}, u32[]{:S(2)}) collective-permute-start(f32[4,4,64,256]{3,2,1,0:T(8,128)S(1)} %bitcast.269), channel_id=1, source_target_pairs={{0,8},{4,12},{8,16},{12,20},{16,24},{20,28},{1,9},{5,13},{9,17},{1... | collective-permute-start | bytes 3145736 | tf_op jit(solution)/shard_map/ppermute | solution.py:26
  248.3 52.3 %collective-permute-start.14 = (f32[4,4,64,256]{3,2,1,0:T(8,128)}, f32[4,4,64,256]{3,2,1,0:T(8,128)}, u32[]{:S(2)}, u32[]{:S(2)}) collective-permute-start(f32[4,4,64,256]{3,2,1,0:T(8,128)} %bitcast.241.rest_15_), channel_id=1, source_target_pairs={{4,0},{8,4},{12,8},{16,12},{20,16},{24,20},{28,24},{5,1},{9,5},{13... | collective-permute-start | bytes 3145736 | tf_op jit(solution)/shard_map/ppermute | solution.py:26
  257.5 43.0 %collective-permute-start.15 = (f32[4,4,64,256]{3,2,1,0:T(8,128)}, f32[4,4,64,256]{3,2,1,0:T(8,128)}, u32[]{:S(2)}, u32[]{:S(2)}) collective-permute-start(f32[4,4,64,256]{3,2,1,0:T(8,128)} %bitcast.241.rest_15_), channel_id=1, source_target_pairs={{8,0},{12,4},{16,8},{20,12},{24,16},{28,20},{9,1},{13,5},{17,9},{2... | collective-permute-start | bytes 3145736 | tf_op jit(solution)/shard_map/ppermute | solution.py:26
  259.6 44.1 %collective-permute-start.16 = (f32[4,4,64,256]{3,2,1,0:T(8,128)}, f32[4,4,64,256]{3,2,1,0:T(8,128)}, u32[]{:S(2)}, u32[]{:S(2)}) collective-permute-start(f32[4,4,64,256]{3,2,1,0:T(8,128)} %bitcast.241.rest_15_), channel_id=1, source_target_pairs={{0,4},{4,8},{8,12},{12,16},{16,20},{20,24},{24,28},{1,5},{5,9},{9,... | collective-permute-start | bytes 3145736 | tf_op jit(solution)/shard_map/ppermute | solution.py:26
  266.4 41.6 %collective-permute-start.17 = (f32[4,4,64,256]{3,2,1,0:T(8,128)}, f32[4,4,64,256]{3,2,1,0:T(8,128)}, u32[]{:S(2)}, u32[]{:S(2)}) collective-permute-start(f32[4,4,64,256]{3,2,1,0:T(8,128)} %bitcast.241.rest_15_), channel_id=1, source_target_pairs={{0,8},{4,12},{8,16},{12,20},{16,24},{20,28},{1,9},{5,13},{9,17},{1... | collective-permute-start | bytes 3145736 | tf_op jit(solution)/shard_map/ppermute | solution.py:26
  (11 other events, 38.3 us)
where the time goes:
time: 328 us; the launch traced here: 322 us
  starting transfers between devices  95.1 us (29%)
  local copies, waits for them, and re-layouts  71.8 us (22%)
  waiting for transfers between devices  57 us (17%)
  Pallas kernels  40.2 us (12%)
  matrix products  28.7 us (9%)
  other arithmetic  26.8 us (8%)
    ppermute x18, starting transfers between devices, passed_along(): lax.ppermute(value, axis, [(source, source + steps) for source in range(f...  54.9 us
    pallas_call x2, Pallas kernels, translate_pairs(): pl.pallas_call(functools.partial(pair_kernel, tuple(offsets), init is not...  40.2 us
    ppermute x18, waiting for transfers between devices, passed_along(): lax.ppermute(value, axis, [(source, source + steps) for source in range(f...  30.6 us
    all_to_all x4, starting transfers between devices, body(): lax.all_to_all(piece, 'dir', split_axis=0, concat_axis=3, tiled=True)  23.5 us
    dot_general x4, matrix products, interpolate(): jnp.einsum('qp,...pu->...qu', phi_map, widened, precision=lax.Precision.H...  17.7 us
    all_to_all x4, starting transfers between devices, body(): lax.all_to_all(summed, 'dir', split_axis=2, concat_axis=0, tiled=True)  16.8 us
    all_to_all x4, waiting for transfers between devices, body(): lax.all_to_all(summed, 'dir', split_axis=2, concat_axis=0, tiled=True)  16.5 us
    gather x8, local copies, waits for them, and re-layouts, body(): jnp.take_along_axis(grouped[c * per_chunk:(c + 1) * per_chunk], by_octant...  12.1 us
  transfers between devices with their start and end apart: 26, of which 14 were waited for; matrix products, arithmetic and copies ran while one was open for 34% of the time, Pallas kernels for 8%

commit v1 on v0

--- a/solution.py
+++ b/solution.py
@@ -93,15 +93,17 @@
         c.start()
     if not has_init:
         acc[...] = jnp.zeros_like(acc)
-    for c in copies:
+    for c in copies[TABLE_PIECES:] if has_init else copies:
         c.wait()
 
-    def item(i, carry):
-        if True:
-            j = order_ref[i]
+    def item(i, carry, low=0, high=classes):
+        j = order_ref[i]
+        k = cls_ref[j]
+
+        @pl.when((k >= low) & (k < high))
+        def _():
             t = tgt_ref[j]
             s = src_ref[j]
-            k = cls_ref[j]
 
             def chunk(j, inner):
                 r0 = pl.multiple_of(j * ROWS, ROWS)
@@ -122,7 +124,14 @@
     if agg_hbm is not None:
         local = pltpu.make_async_copy(sources.at[pl.ds(0, acc.shape[0])], agg_hbm, out_sem.at[1])
         local.start()
-    lax.fori_loop(span_ref[0], span_ref[1], item, 0)
+    if has_init:
+        for p, (a, b) in enumerate(pieces):
+            copies[p].wait()
+            lax.fori_loop(
+                span_ref[0], span_ref[1], functools.partial(item, low=a, high=b), 0
+            )
+    else:
+        lax.fori_loop(span_ref[0], span_ref[1], item, 0)
     done = pltpu.make_async_copy(acc, out_hbm, out_sem.at[0])
     done.start()
     done.wait()

time: 328 us -> 331 us (level)
  the two profiles are of different devices: /device:TPU:22 before, /device:TPU:12 now
where the time goes in v1:
time: 331 us; the launch traced here: 327 us
  starting transfers between devices  95.9 us (29%)
  local copies, waits for them, and re-layouts  71.8 us (22%)
  waiting for transfers between devices  52.2 us (16%)
  Pallas kernels  48.3 us (15%)
  matrix products  28.7 us (9%)
  other arithmetic  26.8 us (8%)
    ppermute x18, starting transfers between devices, passed_along(): lax.ppermute(value, axis, [(source, source + steps) for source in range(f...  63 us
    pallas_call x2, Pallas kernels, translate_pairs(): pl.pallas_call(functools.partial(pair_kernel, tuple(offsets), init is not...  48.3 us
    ppermute x18, waiting for transfers between devices, passed_along(): lax.ppermute(value, axis, [(source, source + steps) for source in range(f...  20.5 us
    all_to_all x4, waiting for transfers between devices, body(): lax.all_to_all(summed, 'dir', split_axis=2, concat_axis=0, tiled=True)  20 us
    all_to_all x4, starting transfers between devices, body(): lax.all_to_all(piece, 'dir', split_axis=0, concat_axis=3, tiled=True)  18.1 us
    dot_general x4, matrix products, interpolate(): jnp.einsum('qp,...pu->...qu', phi_map, widened, precision=lax.Precision.H...  17.7 us
    all_to_all x4, starting transfers between devices, body(): lax.all_to_all(summed, 'dir', split_axis=2, concat_axis=0, tiled=True)  14.8 us
    gather x8, local copies, waits for them, and re-layouts, body(): jnp.take_along_axis(grouped[c * per_chunk:(c + 1) * per_chunk], by_octant...  12.1 us
  transfers between devices with their start and end apart: 26, of which 11 were waited for; matrix products, arithmetic and copies ran while one was open for 34% of the time, Pallas kernels for 9%

profile of v1, /device:TPU:12, one launch (start us, length us, event | category | flops | bytes accessed | tf_op | source)
XLA Modules:
  0.0 326.5 jit_solution(13525683404426252737)
XLA Ops:
  1.7 7.7 %fusion.93 = (f32[32,4,32,128]{3,2,1,0:T(8,128)}, f32[32,4,32,128]{3,2,1,0:T(8,128)}, f32[32,4,32,128]{3,2,1,0:T(8,128)}, f32[32,4,32,128]{3,2,1,0:T(8,128)}) fusion(f32[128,4,32,128]{3,2,1,0:T(8,128)} %param.10), kind=kLoop, calls=%fused_computation.184 | loop fusion | bytes 16777216 | tf_op jit(solution)/shard_map/slice | solution.py:229
  13.2 4.6 %all-to-all-start = ((f32[4,8,4,32,128]{4,3,2,1,0:T(8,128)}), f32[4,8,4,32,128]{4,3,2,1,0:T(8,128)}, u32[]{:S(2)}, u32[]{:S(2)}) async-start(f32[4,8,4,32,128]{4,3,2,1,0:T(8,128)} %broadcast_select_fusion.3), calls=%async_computation | async-start | bytes 4194304 | tf_op jit(solution)/shard_map/all_to_all | solution.py:233
  29.6 8.2 %fusion.94 = (f32[8,256,256]{2,1,0:T(8,128)}, f32[8,256,256]{2,1,0:T(8,128)}) fusion(f32[8,256,256]{2,1,0:T(8,128)S(1)} %copy-done.11), kind=kLoop, calls=%fused_computation.185 | loop fusion | bytes 6291456 | tf_op jit(solution)/shard_map/cos | solution.py:202
  43.5 4.6 %all-to-all-start.2 = ((f32[4,8,4,32,128]{4,3,2,1,0:T(8,128)}), f32[4,8,4,32,128]{4,3,2,1,0:T(8,128)}, u32[]{:S(2)}, u32[]{:S(2)}) async-start(f32[4,8,4,32,128]{4,3,2,1,0:T(8,128)} %broadcast_select_fusion.2), calls=%async_computation.2 | async-start | bytes 4194304 | tf_op jit(solution)/shard_map/all_to_all | solution.py:233
  52.8 4.4 %fusion.19 = f32[8,4,256,256]{3,2,1,0:T(8,128)S(1)} fusion(f32[8,4,128,256]{2,3,1,0:T(8,128)S(1)} %fusion.6, s32[128]{0:T(128)S(1)} %iota_multiply_fusion), kind=kOutput, calls=%fused_computation.54 | convolution fusion | flops 1611333632 | bytes 12583424 | tf_op jit(solution)/shard_map/qp,...pu->...qu/dot_general | solution.py:42
  63.2 10.7 %all-to-all-done.2 = f32[4,8,4,32,128]{4,3,2,1,0:T(8,128)} async-done(((f32[4,8,4,32,128]{4,3,2,1,0:T(8,128)}), f32[4,8,4,32,128]{4,3,2,1,0:T(8,128)}, u32[]{:S(2)}, u32[]{:S(2)}) %all-to-all-start.2) | async-done | bytes 2097184 | tf_op jit(solution)/shard_map/all_to_all | solution.py:233
  77.6 3.6 %gather_fusion.2 = f32[32,4,32,128]{3,2,1,0:T(8,128)} fusion(f32[4,8,4,32,128]{4,3,2,1,0:T(8,128)} %bitcast.258, s32[32]{0:T(128)S(1)} %reshape.417), kind=kCustom, calls=%fused_computation.2.clone | custom fusion | bytes 4194560 | tf_op jit(solution)/shard_map/jit(take_along_axis)/gather | solution.py:228
  87.6 4.3 %all-to-all-done.1 = f32[1,4,256,256]{3,1,0,2:T(4,128)S(1)} async-done(((f32[1,4,256,256]{3,1,0,2:T(4,128)}), f32[1,4,256,256]{3,1,0,2:T(4,128)S(1)}, u32[]{:S(2)}, u32[]{:S(2)}) %all-to-all-start.1) | async-done | bytes 1048608 | tf_op jit(solution)/shard_map/all_to_all | solution.py:246
  92.9 4.4 %all-to-all-start.3 = ((f32[4,8,4,32,128]{4,3,2,1,0:T(8,128)}), f32[4,8,4,32,128]{4,3,2,1,0:T(8,128)}, u32[]{:S(2)}, u32[]{:S(2)}) async-start(f32[4,8,4,32,128]{4,3,2,1,0:T(8,128)} %broadcast_select_fusion.1), calls=%async_computation.3 | async-start | bytes 4194304 | tf_op jit(solution)/shard_map/all_to_all | solution.py:233
  103.2 4.8 %collective-permute-start.4 = (f32[4,4,64,256]{3,2,1,0:T(8,128)S(1)}, f32[4,4,64,256]{3,2,1,0:T(8,128)}, u32[]{:S(2)}, u32[]{:S(2)}) collective-permute-start(f32[4,4,64,256]{3,2,1,0:T(8,128)S(1)} %bitcast.263), channel_id=1, source_target_pairs={{0,4},{4,8},{8,12},{12,16},{16,20},{20,24},{24,28},{1,5},{5,9},{9,... | collective-permute-start | bytes 3145736 | tf_op jit(solution)/shard_map/ppermute | solution.py:26
  108.0 4.8 %collective-permute-start.5 = (f32[4,4,64,256]{3,2,1,0:T(8,128)S(1)}, f32[4,4,64,256]{3,2,1,0:T(8,128)}, u32[]{:S(2)}, u32[]{:S(2)}) collective-permute-start(f32[4,4,64,256]{3,2,1,0:T(8,128)S(1)} %bitcast.264), channel_id=1, source_target_pairs={{0,8},{4,12},{8,16},{12,20},{16,24},{20,28},{1,9},{5,13},{9,17},{1... | collective-permute-start | bytes 3145736 | tf_op jit(solution)/shard_map/ppermute | solution.py:26
  115.6 4.4 %fusion.16 = f32[8,4,256,256]{3,2,1,0:T(8,128)S(1)} fusion(f32[8,4,128,256]{2,3,1,0:T(8,128)S(1)} %fusion.4, s32[128]{0:T(128)S(1)} %iota_multiply_fusion), kind=kOutput, calls=%fused_computation.51 | convolution fusion | flops 1611333632 | bytes 12583424 | tf_op jit(solution)/shard_map/qp,...pu->...qu/dot_general | solution.py:42
  128.2 4.2 %all-to-all-start.4 = ((f32[1,4,256,256]{3,1,0,2:T(4,128)}), f32[1,4,256,256]{3,1,0,2:T(4,128)}, u32[]{:S(2)}, u32[]{:S(2)}) async-start(f32[1,4,256,256]{3,1,0,2:T(4,128)} %copy.112), calls=%async_computation.4 | async-start | bytes 2097152 | tf_op jit(solution)/shard_map/all_to_all | solution.py:246
  132.6 3.6 %gather_fusion.3 = f32[32,4,32,128]{3,2,1,0:T(8,128)} fusion(f32[4,8,4,32,128]{4,3,2,1,0:T(8,128)} %bitcast.257, s32[32]{0:T(128)S(1)} %reshape.422), kind=kCustom, calls=%fused_computation.3.clone | custom fusion | bytes 4194560 | tf_op jit(solution)/shard_map/jit(take_along_axis)/gather | solution.py:228
  142.5 4.4 %all-to-all-done.4 = f32[1,4,256,256]{3,1,0,2:T(4,128)} async-done(((f32[1,4,256,256]{3,1,0,2:T(4,128)}), f32[1,4,256,256]{3,1,0,2:T(4,128)}, u32[]{:S(2)}, u32[]{:S(2)}) %all-to-all-start.4) | async-done | bytes 1048608 | tf_op jit(solution)/shard_map/all_to_all | solution.py:246
  147.0 4.4 %all-to-all-start.5 = ((f32[4,8,4,32,128]{4,3,2,1,0:T(8,128)}), f32[4,8,4,32,128]{4,3,2,1,0:T(8,128)}, u32[]{:S(2)}, u32[]{:S(2)}) async-start(f32[4,8,4,32,128]{4,3,2,1,0:T(8,128)} %broadcast_select_fusion), calls=%async_computation.5 | async-start | bytes 4194304 | tf_op jit(solution)/shard_map/all_to_all | solution.py:233
  158.2 4.8 %collective-permute-start.8 = (f32[4,4,64,256]{3,2,1,0:T(8,128)}, f32[4,4,64,256]{3,2,1,0:T(8,128)}, u32[]{:S(2)}, u32[]{:S(2)}) collective-permute-start(f32[4,4,64,256]{3,2,1,0:T(8,128)} %bitcast.243.rest_5_), channel_id=1, source_target_pairs={{0,4},{4,8},{8,12},{12,16},{16,20},{20,24},{24,28},{1,5},{5,9},{9,... | collective-permute-start | bytes 3145736 | tf_op jit(solution)/shard_map/ppermute | solution.py:26
  163.1 5.0 %collective-permute-start.9 = (f32[4,4,64,256]{3,2,1,0:T(8,128)}, f32[4,4,64,256]{3,2,1,0:T(8,128)}, u32[]{:S(2)}, u32[]{:S(2)}) collective-permute-start(f32[4,4,64,256]{3,2,1,0:T(8,128)} %bitcast.243.rest_5_), channel_id=1, source_target_pairs={{0,8},{4,12},{8,16},{12,20},{16,24},{20,28},{1,9},{5,13},{9,17},{1... | collective-permute-start | bytes 3145736 | tf_op jit(solution)/shard_map/ppermute | solution.py:26
  170.9 4.4 %fusion.13 = f32[8,4,256,256]{3,2,1,0:T(8,128)S(1)} fusion(f32[8,4,128,256]{2,3,1,0:T(8,128)S(1)} %fusion.2, s32[128]{0:T(128)S(1)} %iota_multiply_fusion), kind=kOutput, calls=%fused_computation.48 | convolution fusion | flops 1611333632 | bytes 12583424 | tf_op jit(solution)/shard_map/qp,...pu->...qu/dot_general | solution.py:42
  187.9 11.2 %all-to-all-done.6 = f32[1,4,256,256]{3,1,0,2:T(4,128)S(1)} async-done(((f32[1,4,256,256]{3,1,0,2:T(4,128)}), f32[1,4,256,256]{3,1,0,2:T(4,128)S(1)}, u32[]{:S(2)}, u32[]{:S(2)}) %all-to-all-start.6) | async-done | bytes 1048608 | tf_op jit(solution)/shard_map/all_to_all | solution.py:246
  205.1 4.0 %collective-permute-done.9.rest_9_ = f32[4,4,64,256]{3,2,1,0:T(8,128)} collective-permute-done((f32[4,4,64,256]{3,2,1,0:T(8,128)}, f32[4,4,64,256]{3,2,1,0:T(8,128)}, u32[]{:S(2)}, u32[]{:S(2)}) %collective-permute-start.9) | collective-permute-done | bytes 1048608 | tf_op jit(solution)/shard_map/ppermute | solution.py:26
  212.9 5.0 %collective-permute-start.12 = (f32[4,4,64,256]{3,2,1,0:T(8,128)S(1)}, f32[4,4,64,256]{3,2,1,0:T(8,128)}, u32[]{:S(2)}, u32[]{:S(2)}) collective-permute-start(f32[4,4,64,256]{3,2,1,0:T(8,128)S(1)} %bitcast.268), channel_id=1, source_target_pairs={{0,4},{4,8},{8,12},{12,16},{16,20},{20,24},{24,28},{1,5},{5,9},{9,... | collective-permute-start | bytes 3145736 | tf_op jit(solution)/shard_map/ppermute | solution.py:26
  220.7 4.4 %fusion.10 = f32[8,4,256,256]{3,2,1,0:T(8,128)S(1)} fusion(f32[8,4,128,256]{2,3,1,0:T(8,128)S(1)} %fusion, s32[128]{0:T(128)S(1)} %iota_multiply_fusion), kind=kOutput, calls=%fused_computation.45 | convolution fusion | flops 1611333632 | bytes 12583424 | tf_op jit(solution)/shard_map/qp,...pu->...qu/dot_general | solution.py:42
  228.9 3.5 %all-to-all-start.7 = ((f32[1,4,256,256]{3,1,0,2:T(4,128)}), f32[1,4,256,256]{3,1,0,2:T(4,128)S(1)}, u32[]{:S(2)}, u32[]{:S(2)}) async-start(f32[1,4,256,256]{3,1,0,2:T(4,128)} %copy.128), calls=%async_computation.7 | async-start | bytes 2097152 | tf_op jit(solution)/shard_map/all_to_all | solution.py:246
  233.8 4.9 %collective-permute-start.13 = (f32[4,4,64,256]{3,2,1,0:T(8,128)S(1)}, f32[4,4,64,256]{3,2,1,0:T(8,128)S(1)}, u32[]{:S(2)}, u32[]{:S(2)}) collective-permute-start(f32[4,4,64,256]{3,2,1,0:T(8,128)S(1)} %bitcast.269), channel_id=1, source_target_pairs={{0,8},{4,12},{8,16},{12,20},{16,24},{20,28},{1,9},{5,13},{9,17},{1... | collective-permute-start | bytes 3145736 | tf_op jit(solution)/shard_map/ppermute | solution.py:26
  241.2 4.4 %sort.17 = (s32[768]{0:T(1024)}, s32[768]{0:T(1024)}) sort(s32[768]{0:T(1024)S(1)} %get-tuple-element.59, s32[768]{0:T(1024)S(1)} %iota.36), dimensions={0}, to_apply=%region_1.3 | sort | flops 7680 | bytes 12288 | tf_op jit(solution)/shard_map/jit(argsort)/sort | solution.py:252
  249.9 7.1 %collective-permute-done.10.rest_11_ = f32[4,4,64,256]{3,2,1,0:T(8,128)} collective-permute-done((f32[4,4,64,256]{3,2,1,0:T(8,128)S(1)}, f32[4,4,64,256]{3,2,1,0:T(8,128)}, u32[]{:S(2)}, u32[]{:S(2)}) %collective-permute-start.10) | collective-permute-done | bytes 1048608 | tf_op jit(solution)/shard_map/ppermute | solution.py:26
  259.0 5.9 %collective-permute-start.16 = (f32[4,4,64,256]{3,2,1,0:T(8,128)}, f32[4,4,64,256]{3,2,1,0:T(8,128)}, u32[]{:S(2)}, u32[]{:S(2)}) collective-permute-start(f32[4,4,64,256]{3,2,1,0:T(8,128)} %bitcast.241.rest_15_), channel_id=1, source_target_pairs={{0,4},{4,8},{8,12},{12,16},{16,20},{20,24},{24,28},{1,5},{5,9},{9,... | collective-permute-start | bytes 3145736 | tf_op jit(solution)/shard_map/ppermute | solution.py:26
  264.9 4.7 %collective-permute-start.17 = (f32[4,4,64,256]{3,2,1,0:T(8,128)}, f32[4,4,64,256]{3,2,1,0:T(8,128)}, u32[]{:S(2)}, u32[]{:S(2)}) collective-permute-start(f32[4,4,64,256]{3,2,1,0:T(8,128)} %bitcast.241.rest_15_), channel_id=1, source_target_pairs={{0,8},{4,12},{8,16},{12,20},{16,24},{20,28},{1,9},{5,13},{9,17},{1... | collective-permute-start | bytes 3145736 | tf_op jit(solution)/shard_map/ppermute | solution.py:26
  272.0 30.1 %shard_map.95 = (f32[16,4,64,256]{3,2,1,0:T(8,128)}, f32[16,4,64,256]{3,2,1,0:T(8,128)}) custom-call(s32[768]{0:T(1024)} %pad_add_fusion.1.tgt_ref, s32[768]{0:T(1024)} %get-tuple-element.70.src_ref, s32[768]{0:T(1024)} %pad_add_fusion.3.cls_ref, s32[768]{0:T(1024)} %get-tuple-element.29.order_ref, s32[2]{0:T(128)} %pad_add_fusion.4.span_ref, ...), custom_call_target="tpu_custom_call" | custom-call | flops 1610612736 | bytes 96206848 | tf_op jit(solution)/shard_map/pallas_call | solution.py:154
  303.8 4.3 %collective-permute-done.17.rest_3_ = f32[4,4,64,256]{3,2,1,0:T(8,128)} collective-permute-done((f32[4,4,64,256]{3,2,1,0:T(8,128)}, f32[4,4,64,256]{3,2,1,0:T(8,128)}, u32[]{:S(2)}, u32[]{:S(2)}) %collective-permute-start.17) | collective-permute-done | bytes 1048608 | tf_op jit(solution)/shard_map/ppermute | solution.py:26
  308.1 18.2 %shard_map.96 = f32[16,4,64,256]{3,2,1,0:T(8,128)} custom-call(s32[768]{0:T(1024)} %pad_add_fusion.1.tgt_ref, s32[768]{0:T(1024)} %get-tuple-element.70.src_ref, s32[768]{0:T(1024)} %pad_add_fusion.3.cls_ref, s32[768]{0:T(1024)} %get-tuple-element.29.order_ref, s32[2]{0:T(128)} %pad_add_fusion.5.span_ref, ...), custom_call_target="tpu_custom_call", output_to_operand_aliasing={{}: (10, {})} | custom-call | flops 1610612736 | bytes 45875200 | tf_op jit(solution)/shard_map/pallas_call | solution.py:154
  (137 shorter events, 118.4 us)
Async XLA Ops:
  13.2 4.6 %copy-start.16 = (s32[192]{0:T(256)S(1)}, s32[192]{0:T(256)}, u32[]{:S(2)}) copy-start(s32[192]{0:T(256)} %param.16) | copy-start | bytes 2308
  13.2 30.4 %all-to-all-start = ((f32[4,8,4,32,128]{4,3,2,1,0:T(8,128)}), f32[4,8,4,32,128]{4,3,2,1,0:T(8,128)}, u32[]{:S(2)}, u32[]{:S(2)}) async-start(f32[4,8,4,32,128]{4,3,2,1,0:T(8,128)} %broadcast_select_fusion.3), calls=%async_computation | async-start | bytes 4194304 | tf_op jit(solution)/shard_map/all_to_all | solution.py:233
  17.8 32.2 %collective-permute-start = (s32[4,192]{1,0:T(4,128)S(1)}, s32[4,192]{1,0:T(4,128)S(1)}, u32[]{:S(2)}, u32[]{:S(2)}) collective-permute-start(s32[4,192]{1,0:T(4,128)S(1)} %pad_add_fusion), channel_id=1, source_target_pairs={{0,4},{4,8},{8,12},{12,16},{16,20},{20,24},{24,28},{1,5},{5,9},{9,... | collective-permute-start | bytes 9224 | tf_op jit(solution)/shard_map/ppermute | solution.py:26
  21.3 28.7 %collective-permute-start.1 = (s32[4,192]{1,0:T(4,128)S(1)}, s32[4,192]{1,0:T(4,128)S(1)}, u32[]{:S(2)}, u32[]{:S(2)}) collective-permute-start(s32[4,192]{1,0:T(4,128)S(1)} %pad_add_fusion), channel_id=1, source_target_pairs={{0,8},{4,12},{8,16},{12,20},{16,24},{20,28},{1,9},{5,13},{9,17},{1... | collective-permute-start | bytes 9224 | tf_op jit(solution)/shard_map/ppermute | solution.py:26
  43.5 30.4 %all-to-all-start.2 = ((f32[4,8,4,32,128]{4,3,2,1,0:T(8,128)}), f32[4,8,4,32,128]{4,3,2,1,0:T(8,128)}, u32[]{:S(2)}, u32[]{:S(2)}) async-start(f32[4,8,4,32,128]{4,3,2,1,0:T(8,128)} %broadcast_select_fusion.2), calls=%async_computation.2 | async-start | bytes 4194304 | tf_op jit(solution)/shard_map/all_to_all | solution.py:233
  73.9 18.0 %all-to-all-start.1 = ((f32[1,4,256,256]{3,1,0,2:T(4,128)}), f32[1,4,256,256]{3,1,0,2:T(4,128)S(1)}, u32[]{:S(2)}, u32[]{:S(2)}) async-start(f32[1,4,256,256]{3,1,0,2:T(4,128)} %copy.101), calls=%async_computation.1 | async-start | bytes 2097152 | tf_op jit(solution)/shard_map/all_to_all | solution.py:246
  92.9 35.4 %all-to-all-start.3 = ((f32[4,8,4,32,128]{4,3,2,1,0:T(8,128)}), f32[4,8,4,32,128]{4,3,2,1,0:T(8,128)}, u32[]{:S(2)}, u32[]{:S(2)}) async-start(f32[4,8,4,32,128]{4,3,2,1,0:T(8,128)} %broadcast_select_fusion.1), calls=%async_computation.3 | async-start | bytes 4194304 | tf_op jit(solution)/shard_map/all_to_all | solution.py:233
  97.3 15.5 %copy-start.6 = (f32[1,8,4,4,32,128]{5,4,3,2,1,0:T(8,128)S(1)}, f32[1,8,4,4,32,128]{5,4,3,2,1,0:T(8,128)}, u32[]{:S(2)}) copy-start(f32[1,8,4,4,32,128]{5,4,3,2,1,0:T(8,128)} %copy.105) | copy-start | bytes 6291460
  98.9 16.7 %copy-start.7 = (f32[1,4,4,64,256]{4,3,1,2,0:T(8,128)}, f32[1,4,4,64,256]{4,3,1,2,0:T(8,128)S(1)}, u32[]{:S(2)}) copy-start(f32[1,4,4,64,256]{4,3,1,2,0:T(8,128)S(1)} %copy.159) | copy-start | bytes 3145732
  98.9 55.1 %collective-permute-start.2 = (f32[4,4,64,256]{3,2,1,0:T(8,128)S(1)}, f32[4,4,64,256]{3,2,1,0:T(8,128)}, u32[]{:S(2)}, u32[]{:S(2)}) collective-permute-start(f32[4,4,64,256]{3,2,1,0:T(8,128)S(1)} %bitcast.261), channel_id=1, source_target_pairs={{4,0},{8,4},{12,8},{16,12},{20,16},{24,20},{28,24},{5,1},{9,5},{13... | collective-permute-start | bytes 3145736 | tf_op jit(solution)/shard_map/ppermute | solution.py:26
  101.3 52.7 %collective-permute-start.3 = (f32[4,4,64,256]{3,2,1,0:T(8,128)S(1)}, f32[4,4,64,256]{3,2,1,0:T(8,128)}, u32[]{:S(2)}, u32[]{:S(2)}) collective-permute-start(f32[4,4,64,256]{3,2,1,0:T(8,128)S(1)} %bitcast.262), channel_id=1, source_target_pairs={{8,0},{12,4},{16,8},{20,12},{24,16},{28,20},{9,1},{13,5},{17,9},{2... | collective-permute-start | bytes 3145736 | tf_op jit(solution)/shard_map/ppermute | solution.py:26
  103.2 50.7 %collective-permute-start.4 = (f32[4,4,64,256]{3,2,1,0:T(8,128)S(1)}, f32[4,4,64,256]{3,2,1,0:T(8,128)}, u32[]{:S(2)}, u32[]{:S(2)}) collective-permute-start(f32[4,4,64,256]{3,2,1,0:T(8,128)S(1)} %bitcast.263), channel_id=1, source_target_pairs={{0,4},{4,8},{8,12},{12,16},{16,20},{20,24},{24,28},{1,5},{5,9},{9,... | collective-permute-start | bytes 3145736 | tf_op jit(solution)/shard_map/ppermute | solution.py:26
  108.0 46.0 %collective-permute-start.5 = (f32[4,4,64,256]{3,2,1,0:T(8,128)S(1)}, f32[4,4,64,256]{3,2,1,0:T(8,128)}, u32[]{:S(2)}, u32[]{:S(2)}) collective-permute-start(f32[4,4,64,256]{3,2,1,0:T(8,128)S(1)} %bitcast.264), channel_id=1, source_target_pairs={{0,8},{4,12},{8,16},{12,20},{16,24},{20,28},{1,9},{5,13},{9,17},{1... | collective-permute-start | bytes 3145736 | tf_op jit(solution)/shard_map/ppermute | solution.py:26
  128.2 18.8 %all-to-all-start.4 = ((f32[1,4,256,256]{3,1,0,2:T(4,128)}), f32[1,4,256,256]{3,1,0,2:T(4,128)}, u32[]{:S(2)}, u32[]{:S(2)}) async-start(f32[1,4,256,256]{3,1,0,2:T(4,128)} %copy.112), calls=%async_computation.4 | async-start | bytes 2097152 | tf_op jit(solution)/shard_map/all_to_all | solution.py:246
  147.0 34.2 %all-to-all-start.5 = ((f32[4,8,4,32,128]{4,3,2,1,0:T(8,128)}), f32[4,8,4,32,128]{4,3,2,1,0:T(8,128)}, u32[]{:S(2)}, u32[]{:S(2)}) async-start(f32[4,8,4,32,128]{4,3,2,1,0:T(8,128)} %broadcast_select_fusion), calls=%async_computation.5 | async-start | bytes 4194304 | tf_op jit(solution)/shard_map/all_to_all | solution.py:233
  151.4 16.6 %copy-start.5 = (f32[1,8,4,4,32,128]{5,4,3,2,1,0:T(8,128)S(1)}, f32[1,8,4,4,32,128]{5,4,3,2,1,0:T(8,128)}, u32[]{:S(2)}) copy-start(f32[1,8,4,4,32,128]{5,4,3,2,1,0:T(8,128)} %copy.107) | copy-start | bytes 6291460
  154.0 48.0 %collective-permute-start.6 = (f32[4,4,64,256]{3,2,1,0:T(8,128)}, f32[4,4,64,256]{3,2,1,0:T(8,128)}, u32[]{:S(2)}, u32[]{:S(2)}) collective-permute-start(f32[4,4,64,256]{3,2,1,0:T(8,128)} %bitcast.243.rest_5_), channel_id=1, source_target_pairs={{4,0},{8,4},{12,8},{16,12},{20,16},{24,20},{28,24},{5,1},{9,5},{13... | collective-permute-start | bytes 3145736 | tf_op jit(solution)/shard_map/ppermute | solution.py:26
  155.9 46.1 %collective-permute-start.7 = (f32[4,4,64,256]{3,2,1,0:T(8,128)}, f32[4,4,64,256]{3,2,1,0:T(8,128)}, u32[]{:S(2)}, u32[]{:S(2)}) collective-permute-start(f32[4,4,64,256]{3,2,1,0:T(8,128)} %bitcast.243.rest_5_), channel_id=1, source_target_pairs={{8,0},{12,4},{16,8},{20,12},{24,16},{28,20},{9,1},{13,5},{17,9},{2... | collective-permute-start | bytes 3145736 | tf_op jit(solution)/shard_map/ppermute | solution.py:26
  158.2 46.9 %collective-permute-start.8 = (f32[4,4,64,256]{3,2,1,0:T(8,128)}, f32[4,4,64,256]{3,2,1,0:T(8,128)}, u32[]{:S(2)}, u32[]{:S(2)}) collective-permute-start(f32[4,4,64,256]{3,2,1,0:T(8,128)} %bitcast.243.rest_5_), channel_id=1, source_target_pairs={{0,4},{4,8},{8,12},{12,16},{16,20},{20,24},{24,28},{1,5},{5,9},{9,... | collective-permute-start | bytes 3145736 | tf_op jit(solution)/shard_map/ppermute | solution.py:26
  163.1 46.0 %collective-permute-start.9 = (f32[4,4,64,256]{3,2,1,0:T(8,128)}, f32[4,4,64,256]{3,2,1,0:T(8,128)}, u32[]{:S(2)}, u32[]{:S(2)}) collective-permute-start(f32[4,4,64,256]{3,2,1,0:T(8,128)} %bitcast.243.rest_5_), channel_id=1, source_target_pairs={{0,8},{4,12},{8,16},{12,20},{16,24},{20,28},{1,9},{5,13},{9,17},{1... | collective-permute-start | bytes 3145736 | tf_op jit(solution)/shard_map/ppermute | solution.py:26
  181.2 18.0 %all-to-all-start.6 = ((f32[1,4,256,256]{3,1,0,2:T(4,128)}), f32[1,4,256,256]{3,1,0,2:T(4,128)S(1)}, u32[]{:S(2)}, u32[]{:S(2)}) async-start(f32[1,4,256,256]{3,1,0,2:T(4,128)} %copy.121), calls=%async_computation.6 | async-start | bytes 2097152 | tf_op jit(solution)/shard_map/all_to_all | solution.py:246
  200.2 17.8 %copy-start.4 = (f32[1,8,4,4,32,128]{5,4,3,2,1,0:T(8,128)S(1)}, f32[1,8,4,4,32,128]{5,4,3,2,1,0:T(8,128)}, u32[]{:S(2)}) copy-start(f32[1,8,4,4,32,128]{5,4,3,2,1,0:T(8,128)} %copy.116) | copy-start | bytes 6291460
  201.7 32.1 %copy-start.8 = (f32[1,4,4,64,256]{4,3,1,2,0:T(8,128)}, f32[1,4,4,64,256]{4,3,1,2,0:T(8,128)S(1)}, u32[]{:S(2)}) copy-start(f32[1,4,4,64,256]{4,3,1,2,0:T(8,128)S(1)} %copy.157) | copy-start | bytes 3145732
  209.1 48.0 %collective-permute-start.10 = (f32[4,4,64,256]{3,2,1,0:T(8,128)S(1)}, f32[4,4,64,256]{3,2,1,0:T(8,128)}, u32[]{:S(2)}, u32[]{:S(2)}) collective-permute-start(f32[4,4,64,256]{3,2,1,0:T(8,128)S(1)} %bitcast.266), channel_id=1, source_target_pairs={{4,0},{8,4},{12,8},{16,12},{20,16},{24,20},{28,24},{5,1},{9,5},{13... | collective-permute-start | bytes 3145736 | tf_op jit(solution)/shard_map/ppermute | solution.py:26
  211.0 48.0 %collective-permute-start.11 = (f32[4,4,64,256]{3,2,1,0:T(8,128)S(1)}, f32[4,4,64,256]{3,2,1,0:T(8,128)}, u32[]{:S(2)}, u32[]{:S(2)}) collective-permute-start(f32[4,4,64,256]{3,2,1,0:T(8,128)S(1)} %bitcast.267), channel_id=1, source_target_pairs={{8,0},{12,4},{16,8},{20,12},{24,16},{28,20},{9,1},{13,5},{17,9},{2... | collective-permute-start | bytes 3145736 | tf_op jit(solution)/shard_map/ppermute | solution.py:26
  212.9 52.0 %collective-permute-start.12 = (f32[4,4,64,256]{3,2,1,0:T(8,128)S(1)}, f32[4,4,64,256]{3,2,1,0:T(8,128)}, u32[]{:S(2)}, u32[]{:S(2)}) collective-permute-start(f32[4,4,64,256]{3,2,1,0:T(8,128)S(1)} %bitcast.268), channel_id=1, source_target_pairs={{0,4},{4,8},{8,12},{12,16},{16,20},{20,24},{24,28},{1,5},{5,9},{9,... | collective-permute-start | bytes 3145736 | tf_op jit(solution)/shard_map/ppermute | solution.py:26
  228.9 18.0 %all-to-all-start.7 = ((f32[1,4,256,256]{3,1,0,2:T(4,128)}), f32[1,4,256,256]{3,1,0,2:T(4,128)S(1)}, u32[]{:S(2)}, u32[]{:S(2)}) async-start(f32[1,4,256,256]{3,1,0,2:T(4,128)} %copy.128), calls=%async_computation.7 | async-start | bytes 2097152 | tf_op jit(solution)/shard_map/all_to_all | solution.py:246
  233.8 37.2 %collective-permute-start.13 = (f32[4,4,64,256]{3,2,1,0:T(8,128)S(1)}, f32[4,4,64,256]{3,2,1,0:T(8,128)S(1)}, u32[]{:S(2)}, u32[]{:S(2)}) collective-permute-start(f32[4,4,64,256]{3,2,1,0:T(8,128)S(1)} %bitcast.269), channel_id=1, source_target_pairs={{0,8},{4,12},{8,16},{12,20},{16,24},{20,28},{1,9},{5,13},{9,17},{1... | collective-permute-start | bytes 3145736 | tf_op jit(solution)/shard_map/ppermute | solution.py:26
  248.0 54.1 %collective-permute-start.14 = (f32[4,4,64,256]{3,2,1,0:T(8,128)}, f32[4,4,64,256]{3,2,1,0:T(8,128)}, u32[]{:S(2)}, u32[]{:S(2)}) collective-permute-start(f32[4,4,64,256]{3,2,1,0:T(8,128)} %bitcast.241.rest_15_), channel_id=1, source_target_pairs={{4,0},{8,4},{12,8},{16,12},{20,16},{24,20},{28,24},{5,1},{9,5},{13... | collective-permute-start | bytes 3145736 | tf_op jit(solution)/shard_map/ppermute | solution.py:26
  257.1 45.1 %collective-permute-start.15 = (f32[4,4,64,256]{3,2,1,0:T(8,128)}, f32[4,4,64,256]{3,2,1,0:T(8,128)}, u32[]{:S(2)}, u32[]{:S(2)}) collective-permute-start(f32[4,4,64,256]{3,2,1,0:T(8,128)} %bitcast.241.rest_15_), channel_id=1, source_target_pairs={{8,0},{12,4},{16,8},{20,12},{24,16},{28,20},{9,1},{13,5},{17,9},{2... | collective-permute-start | bytes 3145736 | tf_op jit(solution)/shard_map/ppermute | solution.py:26
  259.0 44.9 %collective-permute-start.16 = (f32[4,4,64,256]{3,2,1,0:T(8,128)}, f32[4,4,64,256]{3,2,1,0:T(8,128)}, u32[]{:S(2)}, u32[]{:S(2)}) collective-permute-start(f32[4,4,64,256]{3,2,1,0:T(8,128)} %bitcast.241.rest_15_), channel_id=1, source_target_pairs={{0,4},{4,8},{8,12},{12,16},{16,20},{20,24},{24,28},{1,5},{5,9},{9,... | collective-permute-start | bytes 3145736 | tf_op jit(solution)/shard_map/ppermute | solution.py:26
  264.9 43.2 %collective-permute-start.17 = (f32[4,4,64,256]{3,2,1,0:T(8,128)}, f32[4,4,64,256]{3,2,1,0:T(8,128)}, u32[]{:S(2)}, u32[]{:S(2)}) collective-permute-start(f32[4,4,64,256]{3,2,1,0:T(8,128)} %bitcast.241.rest_15_), channel_id=1, source_target_pairs={{0,8},{4,12},{8,16},{12,20},{16,24},{20,28},{1,9},{5,13},{9,17},{1... | collective-permute-start | bytes 3145736 | tf_op jit(solution)/shard_map/ppermute | solution.py:26
  (11 other events, 36.9 us)

commit v2 on v0

--- a/solution.py
+++ b/solution.py
@@ -216,11 +216,8 @@
             offsets.append(b * box_dev + c * per_chunk)
 
     for c in range(chunks):
-        piece = jnp.take_along_axis(
-            grouped[c * per_chunk : (c + 1) * per_chunk],
-            by_octant[c * per_chunk : (c + 1) * per_chunk, :, None, None, None],
-            axis=1,
-        )
+        owners = c * per_chunk + jnp.arange(per_chunk, dtype=jnp.int32)
+        piece = grouped[owners[:, None], by_octant[c * per_chunk : (c + 1) * per_chunk]]
         gathered = lax.all_to_all(piece, "dir", split_axis=0, concat_axis=3, tiled=True)
         if c >= 2:
             lo = (c - 2) * (2 * REACH + 1) + 1

time: 328 us -> 324 us (0.988)
  other arithmetic: 26.8 us -> 17.5 us
  matrix products: 28.7 us -> 33.5 us
  Pallas kernels: 40.2 us -> 43.5 us
    gather x8 -> x4, local copies, waits for them, and re-layouts: 12.1 us -> 21.8 us  [body(): grouped[owners[:, None], by_octant[c * per_chunk:(c + 1) * per_chunk]]]
    select_n x4 -> x0, other arithmetic: 9.29 us -> none  [body(): jnp.take_along_axis(grouped[c * per_chunk:(c + 1) * per_chunk], by_octant...]
    slice x6 -> x0, local copies, waits for them, and re-layouts: 8.07 us -> none  [the longest x1 7.67 us: body(): grouped[c * per_chunk:(c + 1) * per_chunk]]
    ppermute x18, waiting for transfers between devices: 30.6 us -> 25.2 us  [passed_along(): lax.ppermute(value, axis, [(source, source + steps) for source in range(f...]
    dot_general x4, matrix products: 11.1 us -> 15.8 us  [interpolate(): jnp.einsum('...t,ut->...u', fields, theta_map, precision=lax.Precision.HIGH)]
    pallas_call x2, Pallas kernels: 40.2 us -> 43.5 us  [translate_pairs(): pl.pallas_call(functools.partial(pair_kernel, tuple(offsets), init is not...]
  transfers between devices with their start and end apart: 26 -> 26, of which waited for: 14 -> 13; matrix products, arithmetic and copies ran while one was open for 34% -> 36% of each run, Pallas kernels for 8% -> 9%
where the time goes in v2:
time: 324 us; the launch traced here: 319 us
  starting transfers between devices  96.4 us (30%)
  local copies, waits for them, and re-layouts  71.6 us (22%)
  waiting for transfers between devices  53.8 us (17%)
  Pallas kernels  43.5 us (13%)
  matrix products  33.5 us (10%)
  other arithmetic  17.5 us (5%)
    ppermute x18, starting transfers between devices, passed_along(): lax.ppermute(value, axis, [(source, source + steps) for source in range(f...  55.9 us
    pallas_call x2, Pallas kernels, translate_pairs(): pl.pallas_call(functools.partial(pair_kernel, tuple(offsets), init is not...  43.5 us
    ppermute x18, waiting for transfers between devices, passed_along(): lax.ppermute(value, axis, [(source, source + steps) for source in range(f...  25.2 us
    all_to_all x4, starting transfers between devices, body(): lax.all_to_all(piece, 'dir', split_axis=0, concat_axis=3, tiled=True)  23.7 us
    gather x4, local copies, waits for them, and re-layouts, body(): grouped[owners[:, None], by_octant[c * per_chunk:(c + 1) * per_chunk]]  21.8 us
    all_to_all x4, waiting for transfers between devices, body(): lax.all_to_all(summed, 'dir', split_axis=2, concat_axis=0, tiled=True)  19.4 us
    dot_general x4, matrix products, interpolate(): jnp.einsum('qp,...pu->...qu', phi_map, widened, precision=lax.Precision.H...  17.7 us
    all_to_all x4, starting transfers between devices, body(): lax.all_to_all(summed, 'dir', split_axis=2, concat_axis=0, tiled=True)  16.8 us
  transfers between devices with their start and end apart: 26, of which 13 were waited for; matrix products, arithmetic and copies ran while one was open for 36% of the time, Pallas kernels for 9%

profile of v2, /device:TPU:22, one launch (start us, length us, event | category | flops | bytes accessed | tf_op | source)
XLA Modules:
  0.0 319.0 jit_solution(12699457616941842750)
XLA Ops:
  1.7 5.5 %gather_fusion = f32[32,4,32,128]{3,2,1,0:T(8,128)} fusion(f32[16,8,4,32,128]{4,3,2,1,0:T(8,128)} %bitcast.218, s32[32]{0:T(128)S(1)} %reshape.384), kind=kCustom, calls=%fused_computation | custom fusion | bytes 4194560 | tf_op jit(solution)/shard_map/gather | solution.py:220
  7.3 4.9 %all-to-all-start = ((f32[4,8,4,32,128]{4,3,2,1,0:T(8,128)}), f32[4,8,4,32,128]{4,3,2,1,0:T(8,128)}, u32[]{:S(2)}, u32[]{:S(2)}) async-start(f32[4,8,4,32,128]{4,3,2,1,0:T(8,128)} %bitcast.6), calls=%async_computation | async-start | bytes 4194304 | tf_op jit(solution)/shard_map/all_to_all | solution.py:221
  17.8 8.2 %fusion.107 = (f32[8,256,256]{2,1,0:T(8,128)}, f32[8,256,256]{2,1,0:T(8,128)}) fusion(f32[8,256,256]{2,1,0:T(8,128)S(1)} %copy-done.8), kind=kLoop, calls=%fused_computation.198 | loop fusion | bytes 6291456 | tf_op jit(solution)/shard_map/cos | solution.py:193
  30.8 5.4 %gather_fusion.1 = f32[32,4,32,128]{3,2,1,0:T(8,128)} fusion(f32[16,8,4,32,128]{4,3,2,1,0:T(8,128)} %bitcast.219, s32[32]{0:T(128)S(1)} %reshape.390), kind=kCustom, calls=%fused_computation.1 | custom fusion | bytes 4194560 | tf_op jit(solution)/shard_map/gather | solution.py:220
  36.4 6.6 %all-to-all-start.2 = ((f32[4,8,4,32,128]{4,3,2,1,0:T(8,128)}), f32[4,8,4,32,128]{4,3,2,1,0:T(8,128)}, u32[]{:S(2)}, u32[]{:S(2)}) async-start(f32[4,8,4,32,128]{4,3,2,1,0:T(8,128)} %bitcast.224), calls=%async_computation.2 | async-start | bytes 4194304 | tf_op jit(solution)/shard_map/all_to_all | solution.py:221
  47.6 4.4 %fusion.19 = f32[8,4,256,256]{3,2,1,0:T(8,128)S(1)} fusion(f32[8,4,128,256]{2,3,1,0:T(8,128)S(1)} %fusion.6, s32[128]{0:T(128)S(1)} %iota_multiply_fusion), kind=kOutput, calls=%fused_computation.50 | convolution fusion | flops 1611333632 | bytes 12583424 | tf_op jit(solution)/shard_map/qp,...pu->...qu/dot_general | solution.py:42
  57.9 9.2 %all-to-all-done.2 = f32[4,8,4,32,128]{4,3,2,1,0:T(8,128)} async-done(((f32[4,8,4,32,128]{4,3,2,1,0:T(8,128)}), f32[4,8,4,32,128]{4,3,2,1,0:T(8,128)}, u32[]{:S(2)}, u32[]{:S(2)}) %all-to-all-start.2) | async-done | bytes 2097184 | tf_op jit(solution)/shard_map/all_to_all | solution.py:221
  67.1 5.2 %all-to-all-start.1 = ((f32[1,4,256,256]{3,1,0,2:T(4,128)}), f32[1,4,256,256]{3,1,0,2:T(4,128)S(1)}, u32[]{:S(2)}, u32[]{:S(2)}) async-start(f32[1,4,256,256]{3,1,0,2:T(4,128)} %copy.97), calls=%async_computation.1 | async-start | bytes 2097152 | tf_op jit(solution)/shard_map/all_to_all | solution.py:234
  72.5 5.4 %gather_fusion.2 = f32[32,4,32,128]{3,2,1,0:T(8,128)} fusion(f32[16,8,4,32,128]{4,3,2,1,0:T(8,128)} %bitcast.220, s32[32]{0:T(128)S(1)} %reshape.396), kind=kCustom, calls=%fused_computation.2 | custom fusion | bytes 4194560 | tf_op jit(solution)/shard_map/gather | solution.py:220
  81.1 4.0 %all-to-all-done.1 = f32[1,4,256,256]{3,1,0,2:T(4,128)S(1)} async-done(((f32[1,4,256,256]{3,1,0,2:T(4,128)}), f32[1,4,256,256]{3,1,0,2:T(4,128)S(1)}, u32[]{:S(2)}, u32[]{:S(2)}) %all-to-all-start.1) | async-done | bytes 1048608 | tf_op jit(solution)/shard_map/all_to_all | solution.py:234
  85.1 6.1 %all-to-all-start.3 = ((f32[4,8,4,32,128]{4,3,2,1,0:T(8,128)}), f32[4,8,4,32,128]{4,3,2,1,0:T(8,128)}, u32[]{:S(2)}, u32[]{:S(2)}) async-start(f32[4,8,4,32,128]{4,3,2,1,0:T(8,128)} %bitcast.223), calls=%async_computation.3 | async-start | bytes 4194304 | tf_op jit(solution)/shard_map/all_to_all | solution.py:221
  97.3 5.3 %collective-permute-start.4 = (f32[4,4,64,256]{3,2,1,0:T(8,128)S(1)}, f32[4,4,64,256]{3,2,1,0:T(8,128)}, u32[]{:S(2)}, u32[]{:S(2)}) collective-permute-start(f32[4,4,64,256]{3,2,1,0:T(8,128)S(1)} %bitcast.227), channel_id=1, source_target_pairs={{0,4},{4,8},{8,12},{12,16},{16,20},{20,24},{24,28},{1,5},{5,9},{9,... | collective-permute-start | bytes 3145736 | tf_op jit(solution)/shard_map/ppermute | solution.py:26
  104.7 4.4 %fusion.4 = f32[8,4,128,256]{2,3,1,0:T(8,128)S(1)} fusion(f32[1,8,4,128,128]{4,3,2,1,0:T(8,128)} %bitcast.216, s32[128]{0:T(128)S(1)} %iota_multiply_fusion), kind=kOutput, calls=%fused_computation.24 | convolution fusion | flops 806027264 | bytes 6291968 | tf_op jit(solution)/shard_map/...t,ut->...u/dot_general | solution.py:41
  109.1 4.4 %fusion.16 = f32[8,4,256,256]{3,2,1,0:T(8,128)S(1)} fusion(f32[8,4,128,256]{2,3,1,0:T(8,128)S(1)} %fusion.4, s32[128]{0:T(128)S(1)} %iota_multiply_fusion), kind=kOutput, calls=%fused_computation.47 | convolution fusion | flops 1611333632 | bytes 12583424 | tf_op jit(solution)/shard_map/qp,...pu->...qu/dot_general | solution.py:42
  121.7 4.3 %all-to-all-start.4 = ((f32[1,4,256,256]{3,1,0,2:T(4,128)}), f32[1,4,256,256]{3,1,0,2:T(4,128)}, u32[]{:S(2)}, u32[]{:S(2)}) async-start(f32[1,4,256,256]{3,1,0,2:T(4,128)} %copy.108), calls=%async_computation.4 | async-start | bytes 2097152 | tf_op jit(solution)/shard_map/all_to_all | solution.py:234
  126.2 5.4 %gather_fusion.3 = f32[32,4,32,128]{3,2,1,0:T(8,128)} fusion(f32[16,8,4,32,128]{4,3,2,1,0:T(8,128)} %bitcast.221, s32[32]{0:T(128)S(1)} %reshape.402), kind=kCustom, calls=%fused_computation.3 | custom fusion | bytes 4194560 | tf_op jit(solution)/shard_map/gather | solution.py:220
  134.7 4.1 %all-to-all-done.4 = f32[1,4,256,256]{3,1,0,2:T(4,128)} async-done(((f32[1,4,256,256]{3,1,0,2:T(4,128)}), f32[1,4,256,256]{3,1,0,2:T(4,128)}, u32[]{:S(2)}, u32[]{:S(2)}) %all-to-all-start.4) | async-done | bytes 1048608 | tf_op jit(solution)/shard_map/all_to_all | solution.py:234
  138.8 6.1 %all-to-all-start.5 = ((f32[4,8,4,32,128]{4,3,2,1,0:T(8,128)}), f32[4,8,4,32,128]{4,3,2,1,0:T(8,128)}, u32[]{:S(2)}, u32[]{:S(2)}) async-start(f32[4,8,4,32,128]{4,3,2,1,0:T(8,128)} %bitcast.222), calls=%async_computation.5 | async-start | bytes 4194304 | tf_op jit(solution)/shard_map/all_to_all | solution.py:221
  153.2 5.8 %collective-permute-start.8 = (f32[4,4,64,256]{3,2,1,0:T(8,128)}, f32[4,4,64,256]{3,2,1,0:T(8,128)}, u32[]{:S(2)}, u32[]{:S(2)}) collective-permute-start(f32[4,4,64,256]{3,2,1,0:T(8,128)} %bitcast.208.rest_5_), channel_id=1, source_target_pairs={{0,4},{4,8},{8,12},{12,16},{16,20},{20,24},{24,28},{1,5},{5,9},{9,... | collective-permute-start | bytes 3145736 | tf_op jit(solution)/shard_map/ppermute | solution.py:26
  161.1 4.4 %fusion.2 = f32[8,4,128,256]{2,3,1,0:T(8,128)S(1)} fusion(f32[1,8,4,128,128]{4,3,2,1,0:T(8,128)} %bitcast.215, s32[128]{0:T(128)S(1)} %iota_multiply_fusion), kind=kOutput, calls=%fused_computation.22 | convolution fusion | flops 806027264 | bytes 6291968 | tf_op jit(solution)/shard_map/...t,ut->...u/dot_general | solution.py:41
  165.5 4.4 %fusion.13 = f32[8,4,256,256]{3,2,1,0:T(8,128)S(1)} fusion(f32[8,4,128,256]{2,3,1,0:T(8,128)S(1)} %fusion.2, s32[128]{0:T(128)S(1)} %iota_multiply_fusion), kind=kOutput, calls=%fused_computation.44 | convolution fusion | flops 1611333632 | bytes 12583424 | tf_op jit(solution)/shard_map/qp,...pu->...qu/dot_general | solution.py:42
  182.6 9.6 %all-to-all-done.6 = f32[1,4,256,256]{3,1,0,2:T(4,128)S(1)} async-done(((f32[1,4,256,256]{3,1,0,2:T(4,128)}), f32[1,4,256,256]{3,1,0,2:T(4,128)S(1)}, u32[]{:S(2)}, u32[]{:S(2)}) %all-to-all-start.6) | async-done | bytes 1048608 | tf_op jit(solution)/shard_map/all_to_all | solution.py:234
  198.1 5.9 %collective-permute-done.9.rest_9_ = f32[4,4,64,256]{3,2,1,0:T(8,128)} collective-permute-done((f32[4,4,64,256]{3,2,1,0:T(8,128)}, f32[4,4,64,256]{3,2,1,0:T(8,128)}, u32[]{:S(2)}, u32[]{:S(2)}) %collective-permute-start.9) | collective-permute-done | bytes 1048608 | tf_op jit(solution)/shard_map/ppermute | solution.py:26
  208.1 6.0 %collective-permute-start.12 = (f32[4,4,64,256]{3,2,1,0:T(8,128)S(1)}, f32[4,4,64,256]{3,2,1,0:T(8,128)}, u32[]{:S(2)}, u32[]{:S(2)}) collective-permute-start(f32[4,4,64,256]{3,2,1,0:T(8,128)S(1)} %bitcast.232), channel_id=1, source_target_pairs={{0,4},{4,8},{8,12},{12,16},{16,20},{20,24},{24,28},{1,5},{5,9},{9,... | collective-permute-start | bytes 3145736 | tf_op jit(solution)/shard_map/ppermute | solution.py:26
  214.1 4.4 %fusion = f32[8,4,128,256]{2,3,1,0:T(8,128)S(1)} fusion(f32[1,8,4,128,128]{4,3,2,1,0:T(8,128)} %bitcast.214, s32[128]{0:T(128)S(1)} %iota_multiply_fusion), kind=kOutput, calls=%fused_computation.20 | convolution fusion | flops 806027264 | bytes 6291968 | tf_op jit(solution)/shard_map/...t,ut->...u/dot_general | solution.py:41
  218.5 4.4 %fusion.10 = f32[8,4,256,256]{3,2,1,0:T(8,128)S(1)} fusion(f32[8,4,128,256]{2,3,1,0:T(8,128)S(1)} %fusion, s32[128]{0:T(128)S(1)} %iota_multiply_fusion), kind=kOutput, calls=%fused_computation.41 | convolution fusion | flops 1611333632 | bytes 12583424 | tf_op jit(solution)/shard_map/qp,...pu->...qu/dot_general | solution.py:42
  236.1 4.4 %sort.17 = (s32[768]{0:T(1024)}, s32[768]{0:T(1024)}) sort(s32[768]{0:T(1024)S(1)} %get-tuple-element.58, s32[768]{0:T(1024)S(1)} %iota.54), dimensions={0}, to_apply=%region_1.2 | sort | flops 7680 | bytes 12288 | tf_op jit(solution)/shard_map/jit(argsort)/sort | solution.py:240
  246.4 5.6 %collective-permute-done.10.rest_11_ = f32[4,4,64,256]{3,2,1,0:T(8,128)} collective-permute-done((f32[4,4,64,256]{3,2,1,0:T(8,128)S(1)}, f32[4,4,64,256]{3,2,1,0:T(8,128)}, u32[]{:S(2)}, u32[]{:S(2)}) %collective-permute-start.10) | collective-permute-done | bytes 1048608 | tf_op jit(solution)/shard_map/ppermute | solution.py:26
  254.2 6.6 %collective-permute-start.16 = (f32[4,4,64,256]{3,2,1,0:T(8,128)}, f32[4,4,64,256]{3,2,1,0:T(8,128)}, u32[]{:S(2)}, u32[]{:S(2)}) collective-permute-start(f32[4,4,64,256]{3,2,1,0:T(8,128)} %bitcast.206.rest_15_), channel_id=1, source_target_pairs={{0,4},{4,8},{8,12},{12,16},{16,20},{20,24},{24,28},{1,5},{5,9},{9,... | collective-permute-start | bytes 3145736 | tf_op jit(solution)/shard_map/ppermute | solution.py:26
  265.1 28.8 %shard_map.95 = (f32[16,4,64,256]{3,2,1,0:T(8,128)}, f32[16,4,64,256]{3,2,1,0:T(8,128)}) custom-call(s32[768]{0:T(1024)} %pad_add_fusion.1.tgt_ref, s32[768]{0:T(1024)} %get-tuple-element.65.src_ref, s32[768]{0:T(1024)} %pad_add_fusion.3.cls_ref, s32[768]{0:T(1024)} %get-tuple-element.28.order_ref, s32[2]{0:T(128)} %pad_add_fusion.4.span_ref, ...), custom_call_target="tpu_custom_call" | custom-call | flops 1610612736 | bytes 96206848 | tf_op jit(solution)/shard_map/pallas_call | solution.py:145
  298.1 5.9 %collective-permute-done.17.rest_3_ = f32[4,4,64,256]{3,2,1,0:T(8,128)} collective-permute-done((f32[4,4,64,256]{3,2,1,0:T(8,128)}, f32[4,4,64,256]{3,2,1,0:T(8,128)}, u32[]{:S(2)}, u32[]{:S(2)}) %collective-permute-start.17) | collective-permute-done | bytes 1048608 | tf_op jit(solution)/shard_map/ppermute | solution.py:26
  304.0 14.7 %shard_map.96 = f32[16,4,64,256]{3,2,1,0:T(8,128)} custom-call(s32[768]{0:T(1024)} %pad_add_fusion.1.tgt_ref, s32[768]{0:T(1024)} %get-tuple-element.65.src_ref, s32[768]{0:T(1024)} %pad_add_fusion.3.cls_ref, s32[768]{0:T(1024)} %get-tuple-element.28.order_ref, s32[2]{0:T(128)} %pad_add_fusion.5.span_ref, ...), custom_call_target="tpu_custom_call", output_to_operand_aliasing={{}: (10, {})} | custom-call | flops 1610612736 | bytes 45875200 | tf_op jit(solution)/shard_map/pallas_call | solution.py:145
  (125 shorter events, 106.7 us)
Async XLA Ops:
  1.7 10.5 %copy-start.11 = (s32[192]{0:T(256)S(1)}, s32[192]{0:T(256)}, u32[]{:S(2)}) copy-start(s32[192]{0:T(256)} %param.13) | copy-start | bytes 2308
  1.7 10.5 %copy-start.12 = (s32[192]{0:T(256)S(1)}, s32[192]{0:T(256)}, u32[]{:S(2)}) copy-start(s32[192]{0:T(256)} %param.12) | copy-start | bytes 2308
  1.7 10.5 %copy-start.13 = (s32[192]{0:T(256)S(1)}, s32[192]{0:T(256)}, u32[]{:S(2)}) copy-start(s32[192]{0:T(256)} %param.14) | copy-start | bytes 2308
  1.7 16.1 %copy-start.8 = (f32[8,256,256]{2,1,0:T(8,128)S(1)}, f32[8,256,256]{2,1,0:T(8,128)}, u32[]{:S(2)}) copy-start(f32[8,256,256]{2,1,0:T(8,128)} %param.10) | copy-start | bytes 6291460
  7.3 29.1 %all-to-all-start = ((f32[4,8,4,32,128]{4,3,2,1,0:T(8,128)}), f32[4,8,4,32,128]{4,3,2,1,0:T(8,128)}, u32[]{:S(2)}, u32[]{:S(2)}) async-start(f32[4,8,4,32,128]{4,3,2,1,0:T(8,128)} %bitcast.6), calls=%async_computation | async-start | bytes 4194304 | tf_op jit(solution)/shard_map/all_to_all | solution.py:221
  12.3 32.5 %collective-permute-start = (s32[4,192]{1,0:T(4,128)S(1)}, s32[4,192]{1,0:T(4,128)S(1)}, u32[]{:S(2)}, u32[]{:S(2)}) collective-permute-start(s32[4,192]{1,0:T(4,128)S(1)} %pad_add_fusion), channel_id=1, source_target_pairs={{0,4},{4,8},{8,12},{12,16},{16,20},{20,24},{24,28},{1,5},{5,9},{9,... | collective-permute-start | bytes 9224 | tf_op jit(solution)/shard_map/ppermute | solution.py:26
  15.7 29.1 %collective-permute-start.1 = (s32[4,192]{1,0:T(4,128)S(1)}, s32[4,192]{1,0:T(4,128)S(1)}, u32[]{:S(2)}, u32[]{:S(2)}) collective-permute-start(s32[4,192]{1,0:T(4,128)S(1)} %pad_add_fusion), channel_id=1, source_target_pairs={{0,8},{4,12},{8,16},{12,20},{16,24},{20,28},{1,9},{5,13},{9,17},{1... | collective-permute-start | bytes 9224 | tf_op jit(solution)/shard_map/ppermute | solution.py:26
  36.4 30.7 %all-to-all-start.2 = ((f32[4,8,4,32,128]{4,3,2,1,0:T(8,128)}), f32[4,8,4,32,128]{4,3,2,1,0:T(8,128)}, u32[]{:S(2)}, u32[]{:S(2)}) async-start(f32[4,8,4,32,128]{4,3,2,1,0:T(8,128)} %bitcast.224), calls=%async_computation.2 | async-start | bytes 4194304 | tf_op jit(solution)/shard_map/all_to_all | solution.py:221
  67.1 18.0 %all-to-all-start.1 = ((f32[1,4,256,256]{3,1,0,2:T(4,128)}), f32[1,4,256,256]{3,1,0,2:T(4,128)S(1)}, u32[]{:S(2)}, u32[]{:S(2)}) async-start(f32[1,4,256,256]{3,1,0,2:T(4,128)} %copy.97), calls=%async_computation.1 | async-start | bytes 2097152 | tf_op jit(solution)/shard_map/all_to_all | solution.py:234
  85.1 36.6 %all-to-all-start.3 = ((f32[4,8,4,32,128]{4,3,2,1,0:T(8,128)}), f32[4,8,4,32,128]{4,3,2,1,0:T(8,128)}, u32[]{:S(2)}, u32[]{:S(2)}) async-start(f32[4,8,4,32,128]{4,3,2,1,0:T(8,128)} %bitcast.223), calls=%async_computation.3 | async-start | bytes 4194304 | tf_op jit(solution)/shard_map/all_to_all | solution.py:221
  92.5 21.0 %copy-start.4 = (f32[1,4,4,64,256]{4,3,1,2,0:T(8,128)}, f32[1,4,4,64,256]{4,3,1,2,0:T(8,128)S(1)}, u32[]{:S(2)}) copy-start(f32[1,4,4,64,256]{4,3,1,2,0:T(8,128)S(1)} %copy.155) | copy-start | bytes 3145732
  92.6 54.7 %collective-permute-start.2 = (f32[4,4,64,256]{3,2,1,0:T(8,128)S(1)}, f32[4,4,64,256]{3,2,1,0:T(8,128)}, u32[]{:S(2)}, u32[]{:S(2)}) collective-permute-start(f32[4,4,64,256]{3,2,1,0:T(8,128)S(1)} %bitcast.225), channel_id=1, source_target_pairs={{4,0},{8,4},{12,8},{16,12},{20,16},{24,20},{28,24},{5,1},{9,5},{13... | collective-permute-start | bytes 3145736 | tf_op jit(solution)/shard_map/ppermute | solution.py:26
  95.0 52.3 %collective-permute-start.3 = (f32[4,4,64,256]{3,2,1,0:T(8,128)S(1)}, f32[4,4,64,256]{3,2,1,0:T(8,128)}, u32[]{:S(2)}, u32[]{:S(2)}) collective-permute-start(f32[4,4,64,256]{3,2,1,0:T(8,128)S(1)} %bitcast.226), channel_id=1, source_target_pairs={{8,0},{12,4},{16,8},{20,12},{24,16},{28,20},{9,1},{13,5},{17,9},{2... | collective-permute-start | bytes 3145736 | tf_op jit(solution)/shard_map/ppermute | solution.py:26
  97.3 50.0 %collective-permute-start.4 = (f32[4,4,64,256]{3,2,1,0:T(8,128)S(1)}, f32[4,4,64,256]{3,2,1,0:T(8,128)}, u32[]{:S(2)}, u32[]{:S(2)}) collective-permute-start(f32[4,4,64,256]{3,2,1,0:T(8,128)S(1)} %bitcast.227), channel_id=1, source_target_pairs={{0,4},{4,8},{8,12},{12,16},{16,20},{20,24},{24,28},{1,5},{5,9},{9,... | collective-permute-start | bytes 3145736 | tf_op jit(solution)/shard_map/ppermute | solution.py:26
  102.6 44.7 %collective-permute-start.5 = (f32[4,4,64,256]{3,2,1,0:T(8,128)S(1)}, f32[4,4,64,256]{3,2,1,0:T(8,128)}, u32[]{:S(2)}, u32[]{:S(2)}) collective-permute-start(f32[4,4,64,256]{3,2,1,0:T(8,128)S(1)} %bitcast.228), channel_id=1, source_target_pairs={{0,8},{4,12},{8,16},{12,20},{16,24},{20,28},{1,9},{5,13},{9,17},{1... | collective-permute-start | bytes 3145736 | tf_op jit(solution)/shard_map/ppermute | solution.py:26
  121.7 17.2 %all-to-all-start.4 = ((f32[1,4,256,256]{3,1,0,2:T(4,128)}), f32[1,4,256,256]{3,1,0,2:T(4,128)}, u32[]{:S(2)}, u32[]{:S(2)}) async-start(f32[1,4,256,256]{3,1,0,2:T(4,128)} %copy.108), calls=%async_computation.4 | async-start | bytes 2097152 | tf_op jit(solution)/shard_map/all_to_all | solution.py:234
  138.8 37.0 %all-to-all-start.5 = ((f32[4,8,4,32,128]{4,3,2,1,0:T(8,128)}), f32[4,8,4,32,128]{4,3,2,1,0:T(8,128)}, u32[]{:S(2)}, u32[]{:S(2)}) async-start(f32[4,8,4,32,128]{4,3,2,1,0:T(8,128)} %bitcast.222), calls=%async_computation.5 | async-start | bytes 4194304 | tf_op jit(solution)/shard_map/all_to_all | solution.py:221
  147.4 48.5 %collective-permute-start.6 = (f32[4,4,64,256]{3,2,1,0:T(8,128)}, f32[4,4,64,256]{3,2,1,0:T(8,128)}, u32[]{:S(2)}, u32[]{:S(2)}) collective-permute-start(f32[4,4,64,256]{3,2,1,0:T(8,128)} %bitcast.208.rest_5_), channel_id=1, source_target_pairs={{4,0},{8,4},{12,8},{16,12},{20,16},{24,20},{28,24},{5,1},{9,5},{13... | collective-permute-start | bytes 3145736 | tf_op jit(solution)/shard_map/ppermute | solution.py:26
  150.4 45.5 %collective-permute-start.7 = (f32[4,4,64,256]{3,2,1,0:T(8,128)}, f32[4,4,64,256]{3,2,1,0:T(8,128)}, u32[]{:S(2)}, u32[]{:S(2)}) collective-permute-start(f32[4,4,64,256]{3,2,1,0:T(8,128)} %bitcast.208.rest_5_), channel_id=1, source_target_pairs={{8,0},{12,4},{16,8},{20,12},{24,16},{28,20},{9,1},{13,5},{17,9},{2... | collective-permute-start | bytes 3145736 | tf_op jit(solution)/shard_map/ppermute | solution.py:26
  153.2 44.9 %collective-permute-start.8 = (f32[4,4,64,256]{3,2,1,0:T(8,128)}, f32[4,4,64,256]{3,2,1,0:T(8,128)}, u32[]{:S(2)}, u32[]{:S(2)}) collective-permute-start(f32[4,4,64,256]{3,2,1,0:T(8,128)} %bitcast.208.rest_5_), channel_id=1, source_target_pairs={{0,4},{4,8},{8,12},{12,16},{16,20},{20,24},{24,28},{1,5},{5,9},{9,... | collective-permute-start | bytes 3145736 | tf_op jit(solution)/shard_map/ppermute | solution.py:26
  159.0 45.0 %collective-permute-start.9 = (f32[4,4,64,256]{3,2,1,0:T(8,128)}, f32[4,4,64,256]{3,2,1,0:T(8,128)}, u32[]{:S(2)}, u32[]{:S(2)}) collective-permute-start(f32[4,4,64,256]{3,2,1,0:T(8,128)} %bitcast.208.rest_5_), channel_id=1, source_target_pairs={{0,8},{4,12},{8,16},{12,20},{16,24},{20,28},{1,9},{5,13},{9,17},{1... | collective-permute-start | bytes 3145736 | tf_op jit(solution)/shard_map/ppermute | solution.py:26
  175.9 16.3 %all-to-all-start.6 = ((f32[1,4,256,256]{3,1,0,2:T(4,128)}), f32[1,4,256,256]{3,1,0,2:T(4,128)S(1)}, u32[]{:S(2)}, u32[]{:S(2)}) async-start(f32[1,4,256,256]{3,1,0,2:T(4,128)} %copy.117), calls=%async_computation.6 | async-start | bytes 2097152 | tf_op jit(solution)/shard_map/all_to_all | solution.py:234
  194.6 37.3 %copy-start.5 = (f32[1,4,4,64,256]{4,3,1,2,0:T(8,128)}, f32[1,4,4,64,256]{4,3,1,2,0:T(8,128)S(1)}, u32[]{:S(2)}) copy-start(f32[1,4,4,64,256]{4,3,1,2,0:T(8,128)S(1)} %copy.153) | copy-start | bytes 3145732
  204.0 48.0 %collective-permute-start.10 = (f32[4,4,64,256]{3,2,1,0:T(8,128)S(1)}, f32[4,4,64,256]{3,2,1,0:T(8,128)}, u32[]{:S(2)}, u32[]{:S(2)}) collective-permute-start(f32[4,4,64,256]{3,2,1,0:T(8,128)S(1)} %bitcast.230), channel_id=1, source_target_pairs={{4,0},{8,4},{12,8},{16,12},{20,16},{24,20},{28,24},{5,1},{9,5},{13... | collective-permute-start | bytes 3145736 | tf_op jit(solution)/shard_map/ppermute | solution.py:26
  205.9 48.3 %collective-permute-start.11 = (f32[4,4,64,256]{3,2,1,0:T(8,128)S(1)}, f32[4,4,64,256]{3,2,1,0:T(8,128)}, u32[]{:S(2)}, u32[]{:S(2)}) collective-permute-start(f32[4,4,64,256]{3,2,1,0:T(8,128)S(1)} %bitcast.231), channel_id=1, source_target_pairs={{8,0},{12,4},{16,8},{20,12},{24,16},{28,20},{9,1},{13,5},{17,9},{2... | collective-permute-start | bytes 3145736 | tf_op jit(solution)/shard_map/ppermute | solution.py:26
  208.1 52.7 %collective-permute-start.12 = (f32[4,4,64,256]{3,2,1,0:T(8,128)S(1)}, f32[4,4,64,256]{3,2,1,0:T(8,128)}, u32[]{:S(2)}, u32[]{:S(2)}) collective-permute-start(f32[4,4,64,256]{3,2,1,0:T(8,128)S(1)} %bitcast.232), channel_id=1, source_target_pairs={{0,4},{4,8},{8,12},{12,16},{16,20},{20,24},{24,28},{1,5},{5,9},{9,... | collective-permute-start | bytes 3145736 | tf_op jit(solution)/shard_map/ppermute | solution.py:26
  226.6 16.6 %all-to-all-start.7 = ((f32[1,4,256,256]{3,1,0,2:T(4,128)}), f32[1,4,256,256]{3,1,0,2:T(4,128)S(1)}, u32[]{:S(2)}, u32[]{:S(2)}) async-start(f32[1,4,256,256]{3,1,0,2:T(4,128)} %copy.124), calls=%async_computation.7 | async-start | bytes 2097152 | tf_op jit(solution)/shard_map/all_to_all | solution.py:234
  231.8 32.2 %collective-permute-start.13 = (f32[4,4,64,256]{3,2,1,0:T(8,128)S(1)}, f32[4,4,64,256]{3,2,1,0:T(8,128)S(1)}, u32[]{:S(2)}, u32[]{:S(2)}) collective-permute-start(f32[4,4,64,256]{3,2,1,0:T(8,128)S(1)} %bitcast.233), channel_id=1, source_target_pairs={{0,8},{4,12},{8,16},{12,20},{16,24},{20,28},{1,9},{5,13},{9,17},{1... | collective-permute-start | bytes 3145736 | tf_op jit(solution)/shard_map/ppermute | solution.py:26
  244.4 50.5 %collective-permute-start.14 = (f32[4,4,64,256]{3,2,1,0:T(8,128)}, f32[4,4,64,256]{3,2,1,0:T(8,128)}, u32[]{:S(2)}, u32[]{:S(2)}) collective-permute-start(f32[4,4,64,256]{3,2,1,0:T(8,128)} %bitcast.206.rest_15_), channel_id=1, source_target_pairs={{4,0},{8,4},{12,8},{16,12},{20,16},{24,20},{28,24},{5,1},{9,5},{13... | collective-permute-start | bytes 3145736 | tf_op jit(solution)/shard_map/ppermute | solution.py:26
  252.0 43.0 %collective-permute-start.15 = (f32[4,4,64,256]{3,2,1,0:T(8,128)}, f32[4,4,64,256]{3,2,1,0:T(8,128)}, u32[]{:S(2)}, u32[]{:S(2)}) collective-permute-start(f32[4,4,64,256]{3,2,1,0:T(8,128)} %bitcast.206.rest_15_), channel_id=1, source_target_pairs={{8,0},{12,4},{16,8},{20,12},{24,16},{28,20},{9,1},{13,5},{17,9},{2... | collective-permute-start | bytes 3145736 | tf_op jit(solution)/shard_map/ppermute | solution.py:26
  254.2 44.0 %collective-permute-start.16 = (f32[4,4,64,256]{3,2,1,0:T(8,128)}, f32[4,4,64,256]{3,2,1,0:T(8,128)}, u32[]{:S(2)}, u32[]{:S(2)}) collective-permute-start(f32[4,4,64,256]{3,2,1,0:T(8,128)} %bitcast.206.rest_15_), channel_id=1, source_target_pairs={{0,4},{4,8},{8,12},{12,16},{16,20},{20,24},{24,28},{1,5},{5,9},{9,... | collective-permute-start | bytes 3145736 | tf_op jit(solution)/shard_map/ppermute | solution.py:26
  260.8 43.2 %collective-permute-start.17 = (f32[4,4,64,256]{3,2,1,0:T(8,128)}, f32[4,4,64,256]{3,2,1,0:T(8,128)}, u32[]{:S(2)}, u32[]{:S(2)}) collective-permute-start(f32[4,4,64,256]{3,2,1,0:T(8,128)} %bitcast.206.rest_15_), channel_id=1, source_target_pairs={{0,8},{4,12},{8,16},{12,20},{16,24},{20,28},{1,9},{5,13},{9,17},{1... | collective-permute-start | bytes 3145736 | tf_op jit(solution)/shard_map/ppermute | solution.py:26
  (8 other events, 36.3 us)

commit v3 on v2

--- a/solution.py
+++ b/solution.py
@@ -13,7 +13,7 @@
 PHI1 = 128
 THETA2 = 256
 PHI2 = 256
-ROWS = 16
+ROWS = 32
 TABLE_PIECES = 4
 
 

time: 324 us -> 323 us (level)
  waiting for transfers between devices: 53.8 us -> 59.2 us
  Pallas kernels: 43.5 us -> 38.3 us
    ppermute x18, waiting for transfers between devices: 25.2 us -> 30.6 us  [passed_along(): lax.ppermute(value, axis, [(source, source + steps) for source in range(f...]
    pallas_call x2, Pallas kernels: 43.5 us -> 38.3 us  [translate_pairs(): pl.pallas_call(functools.partial(pair_kernel, tuple(offsets), init is not...]
  transfers between devices with their start and end apart: 26 -> 26, of which waited for: 13 -> 13; matrix products, arithmetic and copies ran while one was open for 36% -> 36% of each run, Pallas kernels for 9% -> 7%
where the time goes in v3:
time: 323 us; the launch traced here: 319 us
  starting transfers between devices  96.4 us (30%)
  local copies, waits for them, and re-layouts  71.6 us (22%)
  waiting for transfers between devices  59.2 us (18%)
  Pallas kernels  38.3 us (12%)
  matrix products  33.5 us (10%)
  other arithmetic  17.5 us (5%)
    ppermute x18, starting transfers between devices, passed_along(): lax.ppermute(value, axis, [(source, source + steps) for source in range(f...  55.9 us
    pallas_call x2, Pallas kernels, translate_pairs(): pl.pallas_call(functools.partial(pair_kernel, tuple(offsets), init is not...  38.3 us
    ppermute x18, waiting for transfers between devices, passed_along(): lax.ppermute(value, axis, [(source, source + steps) for source in range(f...  30.6 us
    all_to_all x4, starting transfers between devices, body(): lax.all_to_all(piece, 'dir', split_axis=0, concat_axis=3, tiled=True)  23.7 us
    gather x4, local copies, waits for them, and re-layouts, body(): grouped[owners[:, None], by_octant[c * per_chunk:(c + 1) * per_chunk]]  21.8 us
    all_to_all x4, waiting for transfers between devices, body(): lax.all_to_all(summed, 'dir', split_axis=2, concat_axis=0, tiled=True)  19.4 us
    dot_general x4, matrix products, interpolate(): jnp.einsum('qp,...pu->...qu', phi_map, widened, precision=lax.Precision.H...  17.7 us
    all_to_all x4, starting transfers between devices, body(): lax.all_to_all(summed, 'dir', split_axis=2, concat_axis=0, tiled=True)  16.8 us
  transfers between devices with their start and end apart: 26, of which 13 were waited for; matrix products, arithmetic and copies ran while one was open for 36% of the time, Pallas kernels for 7%

profile of v3, /device:TPU:22, one launch (start us, length us, event | category | flops | bytes accessed | tf_op | source)
XLA Modules:
  0.0 319.3 jit_solution(565356513332081840)
XLA Ops:
  1.7 5.5 %gather_fusion = f32[32,4,32,128]{3,2,1,0:T(8,128)} fusion(f32[16,8,4,32,128]{4,3,2,1,0:T(8,128)} %bitcast.218, s32[32]{0:T(128)S(1)} %reshape.384), kind=kCustom, calls=%fused_computation | custom fusion | bytes 4194560 | tf_op jit(solution)/shard_map/gather | solution.py:220
  7.3 4.9 %all-to-all-start = ((f32[4,8,4,32,128]{4,3,2,1,0:T(8,128)}), f32[4,8,4,32,128]{4,3,2,1,0:T(8,128)}, u32[]{:S(2)}, u32[]{:S(2)}) async-start(f32[4,8,4,32,128]{4,3,2,1,0:T(8,128)} %bitcast.6), calls=%async_computation | async-start | bytes 4194304 | tf_op jit(solution)/shard_map/all_to_all | solution.py:221
  17.8 8.2 %fusion.107 = (f32[8,256,256]{2,1,0:T(8,128)}, f32[8,256,256]{2,1,0:T(8,128)}) fusion(f32[8,256,256]{2,1,0:T(8,128)S(1)} %copy-done.8), kind=kLoop, calls=%fused_computation.198 | loop fusion | bytes 6291456 | tf_op jit(solution)/shard_map/cos | solution.py:193
  30.8 5.4 %gather_fusion.1 = f32[32,4,32,128]{3,2,1,0:T(8,128)} fusion(f32[16,8,4,32,128]{4,3,2,1,0:T(8,128)} %bitcast.219, s32[32]{0:T(128)S(1)} %reshape.390), kind=kCustom, calls=%fused_computation.1 | custom fusion | bytes 4194560 | tf_op jit(solution)/shard_map/gather | solution.py:220
  36.4 6.6 %all-to-all-start.2 = ((f32[4,8,4,32,128]{4,3,2,1,0:T(8,128)}), f32[4,8,4,32,128]{4,3,2,1,0:T(8,128)}, u32[]{:S(2)}, u32[]{:S(2)}) async-start(f32[4,8,4,32,128]{4,3,2,1,0:T(8,128)} %bitcast.224), calls=%async_computation.2 | async-start | bytes 4194304 | tf_op jit(solution)/shard_map/all_to_all | solution.py:221
  47.6 4.4 %fusion.19 = f32[8,4,256,256]{3,2,1,0:T(8,128)S(1)} fusion(f32[8,4,128,256]{2,3,1,0:T(8,128)S(1)} %fusion.6, s32[128]{0:T(128)S(1)} %iota_multiply_fusion), kind=kOutput, calls=%fused_computation.50 | convolution fusion | flops 1611333632 | bytes 12583424 | tf_op jit(solution)/shard_map/qp,...pu->...qu/dot_general | solution.py:42
  57.9 9.2 %all-to-all-done.2 = f32[4,8,4,32,128]{4,3,2,1,0:T(8,128)} async-done(((f32[4,8,4,32,128]{4,3,2,1,0:T(8,128)}), f32[4,8,4,32,128]{4,3,2,1,0:T(8,128)}, u32[]{:S(2)}, u32[]{:S(2)}) %all-to-all-start.2) | async-done | bytes 2097184 | tf_op jit(solution)/shard_map/all_to_all | solution.py:221
  67.1 5.2 %all-to-all-start.1 = ((f32[1,4,256,256]{3,1,0,2:T(4,128)}), f32[1,4,256,256]{3,1,0,2:T(4,128)S(1)}, u32[]{:S(2)}, u32[]{:S(2)}) async-start(f32[1,4,256,256]{3,1,0,2:T(4,128)} %copy.97), calls=%async_computation.1 | async-start | bytes 2097152 | tf_op jit(solution)/shard_map/all_to_all | solution.py:234
  72.5 5.4 %gather_fusion.2 = f32[32,4,32,128]{3,2,1,0:T(8,128)} fusion(f32[16,8,4,32,128]{4,3,2,1,0:T(8,128)} %bitcast.220, s32[32]{0:T(128)S(1)} %reshape.396), kind=kCustom, calls=%fused_computation.2 | custom fusion | bytes 4194560 | tf_op jit(solution)/shard_map/gather | solution.py:220
  85.1 6.1 %all-to-all-start.3 = ((f32[4,8,4,32,128]{4,3,2,1,0:T(8,128)}), f32[4,8,4,32,128]{4,3,2,1,0:T(8,128)}, u32[]{:S(2)}, u32[]{:S(2)}) async-start(f32[4,8,4,32,128]{4,3,2,1,0:T(8,128)} %bitcast.223), calls=%async_computation.3 | async-start | bytes 4194304 | tf_op jit(solution)/shard_map/all_to_all | solution.py:221
  97.3 5.3 %collective-permute-start.4 = (f32[4,4,64,256]{3,2,1,0:T(8,128)S(1)}, f32[4,4,64,256]{3,2,1,0:T(8,128)}, u32[]{:S(2)}, u32[]{:S(2)}) collective-permute-start(f32[4,4,64,256]{3,2,1,0:T(8,128)S(1)} %bitcast.227), channel_id=1, source_target_pairs={{0,4},{4,8},{8,12},{12,16},{16,20},{20,24},{24,28},{1,5},{5,9},{9,... | collective-permute-start | bytes 3145736 | tf_op jit(solution)/shard_map/ppermute | solution.py:26
  104.7 4.4 %fusion.4 = f32[8,4,128,256]{2,3,1,0:T(8,128)S(1)} fusion(f32[1,8,4,128,128]{4,3,2,1,0:T(8,128)} %bitcast.216, s32[128]{0:T(128)S(1)} %iota_multiply_fusion), kind=kOutput, calls=%fused_computation.24 | convolution fusion | flops 806027264 | bytes 6291968 | tf_op jit(solution)/shard_map/...t,ut->...u/dot_general | solution.py:41
  109.1 4.4 %fusion.16 = f32[8,4,256,256]{3,2,1,0:T(8,128)S(1)} fusion(f32[8,4,128,256]{2,3,1,0:T(8,128)S(1)} %fusion.4, s32[128]{0:T(128)S(1)} %iota_multiply_fusion), kind=kOutput, calls=%fused_computation.47 | convolution fusion | flops 1611333632 | bytes 12583424 | tf_op jit(solution)/shard_map/qp,...pu->...qu/dot_general | solution.py:42
  121.7 4.3 %all-to-all-start.4 = ((f32[1,4,256,256]{3,1,0,2:T(4,128)}), f32[1,4,256,256]{3,1,0,2:T(4,128)}, u32[]{:S(2)}, u32[]{:S(2)}) async-start(f32[1,4,256,256]{3,1,0,2:T(4,128)} %copy.108), calls=%async_computation.4 | async-start | bytes 2097152 | tf_op jit(solution)/shard_map/all_to_all | solution.py:234
  126.2 5.4 %gather_fusion.3 = f32[32,4,32,128]{3,2,1,0:T(8,128)} fusion(f32[16,8,4,32,128]{4,3,2,1,0:T(8,128)} %bitcast.221, s32[32]{0:T(128)S(1)} %reshape.402), kind=kCustom, calls=%fused_computation.3 | custom fusion | bytes 4194560 | tf_op jit(solution)/shard_map/gather | solution.py:220
  134.7 4.1 %all-to-all-done.4 = f32[1,4,256,256]{3,1,0,2:T(4,128)} async-done(((f32[1,4,256,256]{3,1,0,2:T(4,128)}), f32[1,4,256,256]{3,1,0,2:T(4,128)}, u32[]{:S(2)}, u32[]{:S(2)}) %all-to-all-start.4) | async-done | bytes 1048608 | tf_op jit(solution)/shard_map/all_to_all | solution.py:234
  138.8 6.1 %all-to-all-start.5 = ((f32[4,8,4,32,128]{4,3,2,1,0:T(8,128)}), f32[4,8,4,32,128]{4,3,2,1,0:T(8,128)}, u32[]{:S(2)}, u32[]{:S(2)}) async-start(f32[4,8,4,32,128]{4,3,2,1,0:T(8,128)} %bitcast.222), calls=%async_computation.5 | async-start | bytes 4194304 | tf_op jit(solution)/shard_map/all_to_all | solution.py:221
  153.2 5.8 %collective-permute-start.8 = (f32[4,4,64,256]{3,2,1,0:T(8,128)}, f32[4,4,64,256]{3,2,1,0:T(8,128)}, u32[]{:S(2)}, u32[]{:S(2)}) collective-permute-start(f32[4,4,64,256]{3,2,1,0:T(8,128)} %bitcast.208.rest_5_), channel_id=1, source_target_pairs={{0,4},{4,8},{8,12},{12,16},{16,20},{20,24},{24,28},{1,5},{5,9},{9,... | collective-permute-start | bytes 3145736 | tf_op jit(solution)/shard_map/ppermute | solution.py:26
  161.1 4.4 %fusion.2 = f32[8,4,128,256]{2,3,1,0:T(8,128)S(1)} fusion(f32[1,8,4,128,128]{4,3,2,1,0:T(8,128)} %bitcast.215, s32[128]{0:T(128)S(1)} %iota_multiply_fusion), kind=kOutput, calls=%fused_computation.22 | convolution fusion | flops 806027264 | bytes 6291968 | tf_op jit(solution)/shard_map/...t,ut->...u/dot_general | solution.py:41
  165.5 4.4 %fusion.13 = f32[8,4,256,256]{3,2,1,0:T(8,128)S(1)} fusion(f32[8,4,128,256]{2,3,1,0:T(8,128)S(1)} %fusion.2, s32[128]{0:T(128)S(1)} %iota_multiply_fusion), kind=kOutput, calls=%fused_computation.44 | convolution fusion | flops 1611333632 | bytes 12583424 | tf_op jit(solution)/shard_map/qp,...pu->...qu/dot_general | solution.py:42
  182.6 9.6 %all-to-all-done.6 = f32[1,4,256,256]{3,1,0,2:T(4,128)S(1)} async-done(((f32[1,4,256,256]{3,1,0,2:T(4,128)}), f32[1,4,256,256]{3,1,0,2:T(4,128)S(1)}, u32[]{:S(2)}, u32[]{:S(2)}) %all-to-all-start.6) | async-done | bytes 1048608 | tf_op jit(solution)/shard_map/all_to_all | solution.py:234
  198.1 5.9 %collective-permute-done.9.rest_9_ = f32[4,4,64,256]{3,2,1,0:T(8,128)} collective-permute-done((f32[4,4,64,256]{3,2,1,0:T(8,128)}, f32[4,4,64,256]{3,2,1,0:T(8,128)}, u32[]{:S(2)}, u32[]{:S(2)}) %collective-permute-start.9) | collective-permute-done | bytes 1048608 | tf_op jit(solution)/shard_map/ppermute | solution.py:26
  208.1 6.0 %collective-permute-start.12 = (f32[4,4,64,256]{3,2,1,0:T(8,128)S(1)}, f32[4,4,64,256]{3,2,1,0:T(8,128)}, u32[]{:S(2)}, u32[]{:S(2)}) collective-permute-start(f32[4,4,64,256]{3,2,1,0:T(8,128)S(1)} %bitcast.232), channel_id=1, source_target_pairs={{0,4},{4,8},{8,12},{12,16},{16,20},{20,24},{24,28},{1,5},{5,9},{9,... | collective-permute-start | bytes 3145736 | tf_op jit(solution)/shard_map/ppermute | solution.py:26
  214.1 4.4 %fusion = f32[8,4,128,256]{2,3,1,0:T(8,128)S(1)} fusion(f32[1,8,4,128,128]{4,3,2,1,0:T(8,128)} %bitcast.214, s32[128]{0:T(128)S(1)} %iota_multiply_fusion), kind=kOutput, calls=%fused_computation.20 | convolution fusion | flops 806027264 | bytes 6291968 | tf_op jit(solution)/shard_map/...t,ut->...u/dot_general | solution.py:41
  218.5 4.4 %fusion.10 = f32[8,4,256,256]{3,2,1,0:T(8,128)S(1)} fusion(f32[8,4,128,256]{2,3,1,0:T(8,128)S(1)} %fusion, s32[128]{0:T(128)S(1)} %iota_multiply_fusion), kind=kOutput, calls=%fused_computation.41 | convolution fusion | flops 1611333632 | bytes 12583424 | tf_op jit(solution)/shard_map/qp,...pu->...qu/dot_general | solution.py:42
  236.1 4.4 %sort.17 = (s32[768]{0:T(1024)}, s32[768]{0:T(1024)}) sort(s32[768]{0:T(1024)S(1)} %get-tuple-element.58, s32[768]{0:T(1024)S(1)} %iota.54), dimensions={0}, to_apply=%region_1.2 | sort | flops 7680 | bytes 12288 | tf_op jit(solution)/shard_map/jit(argsort)/sort | solution.py:240
  246.4 5.6 %collective-permute-done.10.rest_11_ = f32[4,4,64,256]{3,2,1,0:T(8,128)} collective-permute-done((f32[4,4,64,256]{3,2,1,0:T(8,128)S(1)}, f32[4,4,64,256]{3,2,1,0:T(8,128)}, u32[]{:S(2)}, u32[]{:S(2)}) %collective-permute-start.10) | collective-permute-done | bytes 1048608 | tf_op jit(solution)/shard_map/ppermute | solution.py:26
  254.2 6.6 %collective-permute-start.16 = (f32[4,4,64,256]{3,2,1,0:T(8,128)}, f32[4,4,64,256]{3,2,1,0:T(8,128)}, u32[]{:S(2)}, u32[]{:S(2)}) collective-permute-start(f32[4,4,64,256]{3,2,1,0:T(8,128)} %bitcast.206.rest_15_), channel_id=1, source_target_pairs={{0,4},{4,8},{8,12},{12,16},{16,20},{20,24},{24,28},{1,5},{5,9},{9,... | collective-permute-start | bytes 3145736 | tf_op jit(solution)/shard_map/ppermute | solution.py:26
  265.1 23.4 %shard_map.95 = (f32[16,4,64,256]{3,2,1,0:T(8,128)}, f32[16,4,64,256]{3,2,1,0:T(8,128)}) custom-call(s32[768]{0:T(1024)} %pad_add_fusion.1.tgt_ref, s32[768]{0:T(1024)} %get-tuple-element.65.src_ref, s32[768]{0:T(1024)} %pad_add_fusion.3.cls_ref, s32[768]{0:T(1024)} %get-tuple-element.28.order_ref, s32[2]{0:T(128)} %pad_add_fusion.4.span_ref, ...), custom_call_target="tpu_custom_call" | custom-call | flops 1610612736 | bytes 96206848 | tf_op jit(solution)/shard_map/pallas_call | solution.py:145
  288.5 6.5 %collective-permute-done.14.rest_0_ = f32[4,4,64,256]{3,2,1,0:T(8,128)} collective-permute-done((f32[4,4,64,256]{3,2,1,0:T(8,128)}, f32[4,4,64,256]{3,2,1,0:T(8,128)}, u32[]{:S(2)}, u32[]{:S(2)}) %collective-permute-start.14) | collective-permute-done | bytes 1048608 | tf_op jit(solution)/shard_map/ppermute | solution.py:26
  298.1 5.9 %collective-permute-done.17.rest_3_ = f32[4,4,64,256]{3,2,1,0:T(8,128)} collective-permute-done((f32[4,4,64,256]{3,2,1,0:T(8,128)}, f32[4,4,64,256]{3,2,1,0:T(8,128)}, u32[]{:S(2)}, u32[]{:S(2)}) %collective-permute-start.17) | collective-permute-done | bytes 1048608 | tf_op jit(solution)/shard_map/ppermute | solution.py:26
  304.0 14.9 %shard_map.96 = f32[16,4,64,256]{3,2,1,0:T(8,128)} custom-call(s32[768]{0:T(1024)} %pad_add_fusion.1.tgt_ref, s32[768]{0:T(1024)} %get-tuple-element.65.src_ref, s32[768]{0:T(1024)} %pad_add_fusion.3.cls_ref, s32[768]{0:T(1024)} %get-tuple-element.28.order_ref, s32[2]{0:T(128)} %pad_add_fusion.5.span_ref, ...), custom_call_target="tpu_custom_call", output_to_operand_aliasing={{}: (10, {})} | custom-call | flops 1610612736 | bytes 45875200 | tf_op jit(solution)/shard_map/pallas_call | solution.py:145
  (125 shorter events, 109.6 us)
Async XLA Ops:
  1.7 10.5 %copy-start.11 = (s32[192]{0:T(256)S(1)}, s32[192]{0:T(256)}, u32[]{:S(2)}) copy-start(s32[192]{0:T(256)} %param.13) | copy-start | bytes 2308
  1.7 10.5 %copy-start.12 = (s32[192]{0:T(256)S(1)}, s32[192]{0:T(256)}, u32[]{:S(2)}) copy-start(s32[192]{0:T(256)} %param.12) | copy-start | bytes 2308
  1.7 10.5 %copy-start.13 = (s32[192]{0:T(256)S(1)}, s32[192]{0:T(256)}, u32[]{:S(2)}) copy-start(s32[192]{0:T(256)} %param.14) | copy-start | bytes 2308
  1.7 16.1 %copy-start.8 = (f32[8,256,256]{2,1,0:T(8,128)S(1)}, f32[8,256,256]{2,1,0:T(8,128)}, u32[]{:S(2)}) copy-start(f32[8,256,256]{2,1,0:T(8,128)} %param.10) | copy-start | bytes 6291460
  7.3 29.1 %all-to-all-start = ((f32[4,8,4,32,128]{4,3,2,1,0:T(8,128)}), f32[4,8,4,32,128]{4,3,2,1,0:T(8,128)}, u32[]{:S(2)}, u32[]{:S(2)}) async-start(f32[4,8,4,32,128]{4,3,2,1,0:T(8,128)} %bitcast.6), calls=%async_computation | async-start | bytes 4194304 | tf_op jit(solution)/shard_map/all_to_all | solution.py:221
  12.3 32.5 %collective-permute-start = (s32[4,192]{1,0:T(4,128)S(1)}, s32[4,192]{1,0:T(4,128)S(1)}, u32[]{:S(2)}, u32[]{:S(2)}) collective-permute-start(s32[4,192]{1,0:T(4,128)S(1)} %pad_add_fusion), channel_id=1, source_target_pairs={{0,4},{4,8},{8,12},{12,16},{16,20},{20,24},{24,28},{1,5},{5,9},{9,... | collective-permute-start | bytes 9224 | tf_op jit(solution)/shard_map/ppermute | solution.py:26
  15.7 29.1 %collective-permute-start.1 = (s32[4,192]{1,0:T(4,128)S(1)}, s32[4,192]{1,0:T(4,128)S(1)}, u32[]{:S(2)}, u32[]{:S(2)}) collective-permute-start(s32[4,192]{1,0:T(4,128)S(1)} %pad_add_fusion), channel_id=1, source_target_pairs={{0,8},{4,12},{8,16},{12,20},{16,24},{20,28},{1,9},{5,13},{9,17},{1... | collective-permute-start | bytes 9224 | tf_op jit(solution)/shard_map/ppermute | solution.py:26
  36.4 30.7 %all-to-all-start.2 = ((f32[4,8,4,32,128]{4,3,2,1,0:T(8,128)}), f32[4,8,4,32,128]{4,3,2,1,0:T(8,128)}, u32[]{:S(2)}, u32[]{:S(2)}) async-start(f32[4,8,4,32,128]{4,3,2,1,0:T(8,128)} %bitcast.224), calls=%async_computation.2 | async-start | bytes 4194304 | tf_op jit(solution)/shard_map/all_to_all | solution.py:221
  67.1 18.0 %all-to-all-start.1 = ((f32[1,4,256,256]{3,1,0,2:T(4,128)}), f32[1,4,256,256]{3,1,0,2:T(4,128)S(1)}, u32[]{:S(2)}, u32[]{:S(2)}) async-start(f32[1,4,256,256]{3,1,0,2:T(4,128)} %copy.97), calls=%async_computation.1 | async-start | bytes 2097152 | tf_op jit(solution)/shard_map/all_to_all | solution.py:234
  85.1 36.6 %all-to-all-start.3 = ((f32[4,8,4,32,128]{4,3,2,1,0:T(8,128)}), f32[4,8,4,32,128]{4,3,2,1,0:T(8,128)}, u32[]{:S(2)}, u32[]{:S(2)}) async-start(f32[4,8,4,32,128]{4,3,2,1,0:T(8,128)} %bitcast.223), calls=%async_computation.3 | async-start | bytes 4194304 | tf_op jit(solution)/shard_map/all_to_all | solution.py:221
  92.5 21.0 %copy-start.4 = (f32[1,4,4,64,256]{4,3,1,2,0:T(8,128)}, f32[1,4,4,64,256]{4,3,1,2,0:T(8,128)S(1)}, u32[]{:S(2)}) copy-start(f32[1,4,4,64,256]{4,3,1,2,0:T(8,128)S(1)} %copy.155) | copy-start | bytes 3145732
  92.6 54.7 %collective-permute-start.2 = (f32[4,4,64,256]{3,2,1,0:T(8,128)S(1)}, f32[4,4,64,256]{3,2,1,0:T(8,128)}, u32[]{:S(2)}, u32[]{:S(2)}) collective-permute-start(f32[4,4,64,256]{3,2,1,0:T(8,128)S(1)} %bitcast.225), channel_id=1, source_target_pairs={{4,0},{8,4},{12,8},{16,12},{20,16},{24,20},{28,24},{5,1},{9,5},{13... | collective-permute-start | bytes 3145736 | tf_op jit(solution)/shard_map/ppermute | solution.py:26
  95.0 52.3 %collective-permute-start.3 = (f32[4,4,64,256]{3,2,1,0:T(8,128)S(1)}, f32[4,4,64,256]{3,2,1,0:T(8,128)}, u32[]{:S(2)}, u32[]{:S(2)}) collective-permute-start(f32[4,4,64,256]{3,2,1,0:T(8,128)S(1)} %bitcast.226), channel_id=1, source_target_pairs={{8,0},{12,4},{16,8},{20,12},{24,16},{28,20},{9,1},{13,5},{17,9},{2... | collective-permute-start | bytes 3145736 | tf_op jit(solution)/shard_map/ppermute | solution.py:26
  97.3 50.0 %collective-permute-start.4 = (f32[4,4,64,256]{3,2,1,0:T(8,128)S(1)}, f32[4,4,64,256]{3,2,1,0:T(8,128)}, u32[]{:S(2)}, u32[]{:S(2)}) collective-permute-start(f32[4,4,64,256]{3,2,1,0:T(8,128)S(1)} %bitcast.227), channel_id=1, source_target_pairs={{0,4},{4,8},{8,12},{12,16},{16,20},{20,24},{24,28},{1,5},{5,9},{9,... | collective-permute-start | bytes 3145736 | tf_op jit(solution)/shard_map/ppermute | solution.py:26
  102.6 44.7 %collective-permute-start.5 = (f32[4,4,64,256]{3,2,1,0:T(8,128)S(1)}, f32[4,4,64,256]{3,2,1,0:T(8,128)}, u32[]{:S(2)}, u32[]{:S(2)}) collective-permute-start(f32[4,4,64,256]{3,2,1,0:T(8,128)S(1)} %bitcast.228), channel_id=1, source_target_pairs={{0,8},{4,12},{8,16},{12,20},{16,24},{20,28},{1,9},{5,13},{9,17},{1... | collective-permute-start | bytes 3145736 | tf_op jit(solution)/shard_map/ppermute | solution.py:26
  121.7 17.2 %all-to-all-start.4 = ((f32[1,4,256,256]{3,1,0,2:T(4,128)}), f32[1,4,256,256]{3,1,0,2:T(4,128)}, u32[]{:S(2)}, u32[]{:S(2)}) async-start(f32[1,4,256,256]{3,1,0,2:T(4,128)} %copy.108), calls=%async_computation.4 | async-start | bytes 2097152 | tf_op jit(solution)/shard_map/all_to_all | solution.py:234
  138.8 37.0 %all-to-all-start.5 = ((f32[4,8,4,32,128]{4,3,2,1,0:T(8,128)}), f32[4,8,4,32,128]{4,3,2,1,0:T(8,128)}, u32[]{:S(2)}, u32[]{:S(2)}) async-start(f32[4,8,4,32,128]{4,3,2,1,0:T(8,128)} %bitcast.222), calls=%async_computation.5 | async-start | bytes 4194304 | tf_op jit(solution)/shard_map/all_to_all | solution.py:221
  147.4 48.5 %collective-permute-start.6 = (f32[4,4,64,256]{3,2,1,0:T(8,128)}, f32[4,4,64,256]{3,2,1,0:T(8,128)}, u32[]{:S(2)}, u32[]{:S(2)}) collective-permute-start(f32[4,4,64,256]{3,2,1,0:T(8,128)} %bitcast.208.rest_5_), channel_id=1, source_target_pairs={{4,0},{8,4},{12,8},{16,12},{20,16},{24,20},{28,24},{5,1},{9,5},{13... | collective-permute-start | bytes 3145736 | tf_op jit(solution)/shard_map/ppermute | solution.py:26
  150.4 45.5 %collective-permute-start.7 = (f32[4,4,64,256]{3,2,1,0:T(8,128)}, f32[4,4,64,256]{3,2,1,0:T(8,128)}, u32[]{:S(2)}, u32[]{:S(2)}) collective-permute-start(f32[4,4,64,256]{3,2,1,0:T(8,128)} %bitcast.208.rest_5_), channel_id=1, source_target_pairs={{8,0},{12,4},{16,8},{20,12},{24,16},{28,20},{9,1},{13,5},{17,9},{2... | collective-permute-start | bytes 3145736 | tf_op jit(solution)/shard_map/ppermute | solution.py:26
  153.2 44.9 %collective-permute-start.8 = (f32[4,4,64,256]{3,2,1,0:T(8,128)}, f32[4,4,64,256]{3,2,1,0:T(8,128)}, u32[]{:S(2)}, u32[]{:S(2)}) collective-permute-start(f32[4,4,64,256]{3,2,1,0:T(8,128)} %bitcast.208.rest_5_), channel_id=1, source_target_pairs={{0,4},{4,8},{8,12},{12,16},{16,20},{20,24},{24,28},{1,5},{5,9},{9,... | collective-permute-start | bytes 3145736 | tf_op jit(solution)/shard_map/ppermute | solution.py:26
  159.0 45.0 %collective-permute-start.9 = (f32[4,4,64,256]{3,2,1,0:T(8,128)}, f32[4,4,64,256]{3,2,1,0:T(8,128)}, u32[]{:S(2)}, u32[]{:S(2)}) collective-permute-start(f32[4,4,64,256]{3,2,1,0:T(8,128)} %bitcast.208.rest_5_), channel_id=1, source_target_pairs={{0,8},{4,12},{8,16},{12,20},{16,24},{20,28},{1,9},{5,13},{9,17},{1... | collective-permute-start | bytes 3145736 | tf_op jit(solution)/shard_map/ppermute | solution.py:26
  175.9 16.3 %all-to-all-start.6 = ((f32[1,4,256,256]{3,1,0,2:T(4,128)}), f32[1,4,256,256]{3,1,0,2:T(4,128)S(1)}, u32[]{:S(2)}, u32[]{:S(2)}) async-start(f32[1,4,256,256]{3,1,0,2:T(4,128)} %copy.117), calls=%async_computation.6 | async-start | bytes 2097152 | tf_op jit(solution)/shard_map/all_to_all | solution.py:234
  194.6 37.3 %copy-start.5 = (f32[1,4,4,64,256]{4,3,1,2,0:T(8,128)}, f32[1,4,4,64,256]{4,3,1,2,0:T(8,128)S(1)}, u32[]{:S(2)}) copy-start(f32[1,4,4,64,256]{4,3,1,2,0:T(8,128)S(1)} %copy.153) | copy-start | bytes 3145732
  204.0 48.0 %collective-permute-start.10 = (f32[4,4,64,256]{3,2,1,0:T(8,128)S(1)}, f32[4,4,64,256]{3,2,1,0:T(8,128)}, u32[]{:S(2)}, u32[]{:S(2)}) collective-permute-start(f32[4,4,64,256]{3,2,1,0:T(8,128)S(1)} %bitcast.230), channel_id=1, source_target_pairs={{4,0},{8,4},{12,8},{16,12},{20,16},{24,20},{28,24},{5,1},{9,5},{13... | collective-permute-start | bytes 3145736 | tf_op jit(solution)/shard_map/ppermute | solution.py:26
  205.9 48.3 %collective-permute-start.11 = (f32[4,4,64,256]{3,2,1,0:T(8,128)S(1)}, f32[4,4,64,256]{3,2,1,0:T(8,128)}, u32[]{:S(2)}, u32[]{:S(2)}) collective-permute-start(f32[4,4,64,256]{3,2,1,0:T(8,128)S(1)} %bitcast.231), channel_id=1, source_target_pairs={{8,0},{12,4},{16,8},{20,12},{24,16},{28,20},{9,1},{13,5},{17,9},{2... | collective-permute-start | bytes 3145736 | tf_op jit(solution)/shard_map/ppermute | solution.py:26
  208.1 52.7 %collective-permute-start.12 = (f32[4,4,64,256]{3,2,1,0:T(8,128)S(1)}, f32[4,4,64,256]{3,2,1,0:T(8,128)}, u32[]{:S(2)}, u32[]{:S(2)}) collective-permute-start(f32[4,4,64,256]{3,2,1,0:T(8,128)S(1)} %bitcast.232), channel_id=1, source_target_pairs={{0,4},{4,8},{8,12},{12,16},{16,20},{20,24},{24,28},{1,5},{5,9},{9,... | collective-permute-start | bytes 3145736 | tf_op jit(solution)/shard_map/ppermute | solution.py:26
  226.6 16.6 %all-to-all-start.7 = ((f32[1,4,256,256]{3,1,0,2:T(4,128)}), f32[1,4,256,256]{3,1,0,2:T(4,128)S(1)}, u32[]{:S(2)}, u32[]{:S(2)}) async-start(f32[1,4,256,256]{3,1,0,2:T(4,128)} %copy.124), calls=%async_computation.7 | async-start | bytes 2097152 | tf_op jit(solution)/shard_map/all_to_all | solution.py:234
  231.8 32.2 %collective-permute-start.13 = (f32[4,4,64,256]{3,2,1,0:T(8,128)S(1)}, f32[4,4,64,256]{3,2,1,0:T(8,128)S(1)}, u32[]{:S(2)}, u32[]{:S(2)}) collective-permute-start(f32[4,4,64,256]{3,2,1,0:T(8,128)S(1)} %bitcast.233), channel_id=1, source_target_pairs={{0,8},{4,12},{8,16},{12,20},{16,24},{20,28},{1,9},{5,13},{9,17},{1... | collective-permute-start | bytes 3145736 | tf_op jit(solution)/shard_map/ppermute | solution.py:26
  244.4 50.5 %collective-permute-start.14 = (f32[4,4,64,256]{3,2,1,0:T(8,128)}, f32[4,4,64,256]{3,2,1,0:T(8,128)}, u32[]{:S(2)}, u32[]{:S(2)}) collective-permute-start(f32[4,4,64,256]{3,2,1,0:T(8,128)} %bitcast.206.rest_15_), channel_id=1, source_target_pairs={{4,0},{8,4},{12,8},{16,12},{20,16},{24,20},{28,24},{5,1},{9,5},{13... | collective-permute-start | bytes 3145736 | tf_op jit(solution)/shard_map/ppermute | solution.py:26
  252.0 43.0 %collective-permute-start.15 = (f32[4,4,64,256]{3,2,1,0:T(8,128)}, f32[4,4,64,256]{3,2,1,0:T(8,128)}, u32[]{:S(2)}, u32[]{:S(2)}) collective-permute-start(f32[4,4,64,256]{3,2,1,0:T(8,128)} %bitcast.206.rest_15_), channel_id=1, source_target_pairs={{8,0},{12,4},{16,8},{20,12},{24,16},{28,20},{9,1},{13,5},{17,9},{2... | collective-permute-start | bytes 3145736 | tf_op jit(solution)/shard_map/ppermute | solution.py:26
  254.2 44.0 %collective-permute-start.16 = (f32[4,4,64,256]{3,2,1,0:T(8,128)}, f32[4,4,64,256]{3,2,1,0:T(8,128)}, u32[]{:S(2)}, u32[]{:S(2)}) collective-permute-start(f32[4,4,64,256]{3,2,1,0:T(8,128)} %bitcast.206.rest_15_), channel_id=1, source_target_pairs={{0,4},{4,8},{8,12},{12,16},{16,20},{20,24},{24,28},{1,5},{5,9},{9,... | collective-permute-start | bytes 3145736 | tf_op jit(solution)/shard_map/ppermute | solution.py:26
  260.8 43.2 %collective-permute-start.17 = (f32[4,4,64,256]{3,2,1,0:T(8,128)}, f32[4,4,64,256]{3,2,1,0:T(8,128)}, u32[]{:S(2)}, u32[]{:S(2)}) collective-permute-start(f32[4,4,64,256]{3,2,1,0:T(8,128)} %bitcast.206.rest_15_), channel_id=1, source_target_pairs={{0,8},{4,12},{8,16},{12,20},{16,24},{20,28},{1,9},{5,13},{9,17},{1... | collective-permute-start | bytes 3145736 | tf_op jit(solution)/shard_map/ppermute | solution.py:26
  (8 other events, 36.3 us)

commit v4 on v3

--- a/solution.py
+++ b/solution.py
@@ -14,7 +14,7 @@
 THETA2 = 256
 PHI2 = 256
 ROWS = 32
-TABLE_PIECES = 4
+TABLE_PIECES = 8
 
 
 HIGHEST = lax.Precision.HIGHEST

time: 323 us -> 323 us (level)
  Pallas kernels: 38.3 us -> 34.9 us
    pallas_call x2, Pallas kernels: 38.3 us -> 34.9 us  [translate_pairs(): pl.pallas_call(functools.partial(pair_kernel, tuple(offsets), init is not...]
where the time goes in v4:
time: 323 us; the launch traced here: 318 us
  starting transfers between devices  96.4 us (30%)
  local copies, waits for them, and re-layouts  71.6 us (22%)
  waiting for transfers between devices  61.3 us (19%)
  Pallas kernels  34.9 us (11%)
  matrix products  33.5 us (10%)
  other arithmetic  17.5 us (5%)
    ppermute x18, starting transfers between devices, passed_along(): lax.ppermute(value, axis, [(source, source + steps) for source in range(f...  55.9 us
    pallas_call x2, Pallas kernels, translate_pairs(): pl.pallas_call(functools.partial(pair_kernel, tuple(offsets), init is not...  34.9 us
    ppermute x18, waiting for transfers between devices, passed_along(): lax.ppermute(value, axis, [(source, source + steps) for source in range(f...  32.6 us
    all_to_all x4, starting transfers between devices, body(): lax.all_to_all(piece, 'dir', split_axis=0, concat_axis=3, tiled=True)  23.7 us
    gather x4, local copies, waits for them, and re-layouts, body(): grouped[owners[:, None], by_octant[c * per_chunk:(c + 1) * per_chunk]]  21.8 us
    all_to_all x4, waiting for transfers between devices, body(): lax.all_to_all(summed, 'dir', split_axis=2, concat_axis=0, tiled=True)  19.4 us
    dot_general x4, matrix products, interpolate(): jnp.einsum('qp,...pu->...qu', phi_map, widened, precision=lax.Precision.H...  17.7 us
    all_to_all x4, starting transfers between devices, body(): lax.all_to_all(summed, 'dir', split_axis=2, concat_axis=0, tiled=True)  16.8 us
  transfers between devices with their start and end apart: 26, of which 13 were waited for; matrix products, arithmetic and copies ran while one was open for 36% of the time, Pallas kernels for 7%

profile of v4, /device:TPU:22, one launch (start us, length us, event | category | flops | bytes accessed | tf_op | source)
XLA Modules:
  0.0 317.9 jit_solution(6431537247115343552)
XLA Ops:
  1.7 5.5 %gather_fusion = f32[32,4,32,128]{3,2,1,0:T(8,128)} fusion(f32[16,8,4,32,128]{4,3,2,1,0:T(8,128)} %bitcast.218, s32[32]{0:T(128)S(1)} %reshape.384), kind=kCustom, calls=%fused_computation | custom fusion | bytes 4194560 | tf_op jit(solution)/shard_map/gather | solution.py:220
  7.3 4.9 %all-to-all-start = ((f32[4,8,4,32,128]{4,3,2,1,0:T(8,128)}), f32[4,8,4,32,128]{4,3,2,1,0:T(8,128)}, u32[]{:S(2)}, u32[]{:S(2)}) async-start(f32[4,8,4,32,128]{4,3,2,1,0:T(8,128)} %bitcast.6), calls=%async_computation | async-start | bytes 4194304 | tf_op jit(solution)/shard_map/all_to_all | solution.py:221
  17.8 8.2 %fusion.107 = (f32[8,256,256]{2,1,0:T(8,128)}, f32[8,256,256]{2,1,0:T(8,128)}) fusion(f32[8,256,256]{2,1,0:T(8,128)S(1)} %copy-done.8), kind=kLoop, calls=%fused_computation.198 | loop fusion | bytes 6291456 | tf_op jit(solution)/shard_map/cos | solution.py:193
  30.8 5.4 %gather_fusion.1 = f32[32,4,32,128]{3,2,1,0:T(8,128)} fusion(f32[16,8,4,32,128]{4,3,2,1,0:T(8,128)} %bitcast.219, s32[32]{0:T(128)S(1)} %reshape.390), kind=kCustom, calls=%fused_computation.1 | custom fusion | bytes 4194560 | tf_op jit(solution)/shard_map/gather | solution.py:220
  36.4 6.6 %all-to-all-start.2 = ((f32[4,8,4,32,128]{4,3,2,1,0:T(8,128)}), f32[4,8,4,32,128]{4,3,2,1,0:T(8,128)}, u32[]{:S(2)}, u32[]{:S(2)}) async-start(f32[4,8,4,32,128]{4,3,2,1,0:T(8,128)} %bitcast.224), calls=%async_computation.2 | async-start | bytes 4194304 | tf_op jit(solution)/shard_map/all_to_all | solution.py:221
  47.6 4.4 %fusion.19 = f32[8,4,256,256]{3,2,1,0:T(8,128)S(1)} fusion(f32[8,4,128,256]{2,3,1,0:T(8,128)S(1)} %fusion.6, s32[128]{0:T(128)S(1)} %iota_multiply_fusion), kind=kOutput, calls=%fused_computation.50 | convolution fusion | flops 1611333632 | bytes 12583424 | tf_op jit(solution)/shard_map/qp,...pu->...qu/dot_general | solution.py:42
  57.9 9.2 %all-to-all-done.2 = f32[4,8,4,32,128]{4,3,2,1,0:T(8,128)} async-done(((f32[4,8,4,32,128]{4,3,2,1,0:T(8,128)}), f32[4,8,4,32,128]{4,3,2,1,0:T(8,128)}, u32[]{:S(2)}, u32[]{:S(2)}) %all-to-all-start.2) | async-done | bytes 2097184 | tf_op jit(solution)/shard_map/all_to_all | solution.py:221
  67.1 5.2 %all-to-all-start.1 = ((f32[1,4,256,256]{3,1,0,2:T(4,128)}), f32[1,4,256,256]{3,1,0,2:T(4,128)S(1)}, u32[]{:S(2)}, u32[]{:S(2)}) async-start(f32[1,4,256,256]{3,1,0,2:T(4,128)} %copy.97), calls=%async_computation.1 | async-start | bytes 2097152 | tf_op jit(solution)/shard_map/all_to_all | solution.py:234
  72.5 5.4 %gather_fusion.2 = f32[32,4,32,128]{3,2,1,0:T(8,128)} fusion(f32[16,8,4,32,128]{4,3,2,1,0:T(8,128)} %bitcast.220, s32[32]{0:T(128)S(1)} %reshape.396), kind=kCustom, calls=%fused_computation.2 | custom fusion | bytes 4194560 | tf_op jit(solution)/shard_map/gather | solution.py:220
  85.1 6.1 %all-to-all-start.3 = ((f32[4,8,4,32,128]{4,3,2,1,0:T(8,128)}), f32[4,8,4,32,128]{4,3,2,1,0:T(8,128)}, u32[]{:S(2)}, u32[]{:S(2)}) async-start(f32[4,8,4,32,128]{4,3,2,1,0:T(8,128)} %bitcast.223), calls=%async_computation.3 | async-start | bytes 4194304 | tf_op jit(solution)/shard_map/all_to_all | solution.py:221
  97.3 5.3 %collective-permute-start.4 = (f32[4,4,64,256]{3,2,1,0:T(8,128)S(1)}, f32[4,4,64,256]{3,2,1,0:T(8,128)}, u32[]{:S(2)}, u32[]{:S(2)}) collective-permute-start(f32[4,4,64,256]{3,2,1,0:T(8,128)S(1)} %bitcast.227), channel_id=1, source_target_pairs={{0,4},{4,8},{8,12},{12,16},{16,20},{20,24},{24,28},{1,5},{5,9},{9,... | collective-permute-start | bytes 3145736 | tf_op jit(solution)/shard_map/ppermute | solution.py:26
  104.7 4.4 %fusion.4 = f32[8,4,128,256]{2,3,1,0:T(8,128)S(1)} fusion(f32[1,8,4,128,128]{4,3,2,1,0:T(8,128)} %bitcast.216, s32[128]{0:T(128)S(1)} %iota_multiply_fusion), kind=kOutput, calls=%fused_computation.24 | convolution fusion | flops 806027264 | bytes 6291968 | tf_op jit(solution)/shard_map/...t,ut->...u/dot_general | solution.py:41
  109.1 4.4 %fusion.16 = f32[8,4,256,256]{3,2,1,0:T(8,128)S(1)} fusion(f32[8,4,128,256]{2,3,1,0:T(8,128)S(1)} %fusion.4, s32[128]{0:T(128)S(1)} %iota_multiply_fusion), kind=kOutput, calls=%fused_computation.47 | convolution fusion | flops 1611333632 | bytes 12583424 | tf_op jit(solution)/shard_map/qp,...pu->...qu/dot_general | solution.py:42
  121.7 4.3 %all-to-all-start.4 = ((f32[1,4,256,256]{3,1,0,2:T(4,128)}), f32[1,4,256,256]{3,1,0,2:T(4,128)}, u32[]{:S(2)}, u32[]{:S(2)}) async-start(f32[1,4,256,256]{3,1,0,2:T(4,128)} %copy.108), calls=%async_computation.4 | async-start | bytes 2097152 | tf_op jit(solution)/shard_map/all_to_all | solution.py:234
  126.2 5.4 %gather_fusion.3 = f32[32,4,32,128]{3,2,1,0:T(8,128)} fusion(f32[16,8,4,32,128]{4,3,2,1,0:T(8,128)} %bitcast.221, s32[32]{0:T(128)S(1)} %reshape.402), kind=kCustom, calls=%fused_computation.3 | custom fusion | bytes 4194560 | tf_op jit(solution)/shard_map/gather | solution.py:220
  134.7 4.1 %all-to-all-done.4 = f32[1,4,256,256]{3,1,0,2:T(4,128)} async-done(((f32[1,4,256,256]{3,1,0,2:T(4,128)}), f32[1,4,256,256]{3,1,0,2:T(4,128)}, u32[]{:S(2)}, u32[]{:S(2)}) %all-to-all-start.4) | async-done | bytes 1048608 | tf_op jit(solution)/shard_map/all_to_all | solution.py:234
  138.8 6.1 %all-to-all-start.5 = ((f32[4,8,4,32,128]{4,3,2,1,0:T(8,128)}), f32[4,8,4,32,128]{4,3,2,1,0:T(8,128)}, u32[]{:S(2)}, u32[]{:S(2)}) async-start(f32[4,8,4,32,128]{4,3,2,1,0:T(8,128)} %bitcast.222), calls=%async_computation.5 | async-start | bytes 4194304 | tf_op jit(solution)/shard_map/all_to_all | solution.py:221
  153.2 5.8 %collective-permute-start.8 = (f32[4,4,64,256]{3,2,1,0:T(8,128)}, f32[4,4,64,256]{3,2,1,0:T(8,128)}, u32[]{:S(2)}, u32[]{:S(2)}) collective-permute-start(f32[4,4,64,256]{3,2,1,0:T(8,128)} %bitcast.208.rest_5_), channel_id=1, source_target_pairs={{0,4},{4,8},{8,12},{12,16},{16,20},{20,24},{24,28},{1,5},{5,9},{9,... | collective-permute-start | bytes 3145736 | tf_op jit(solution)/shard_map/ppermute | solution.py:26
  161.1 4.4 %fusion.2 = f32[8,4,128,256]{2,3,1,0:T(8,128)S(1)} fusion(f32[1,8,4,128,128]{4,3,2,1,0:T(8,128)} %bitcast.215, s32[128]{0:T(128)S(1)} %iota_multiply_fusion), kind=kOutput, calls=%fused_computation.22 | convolution fusion | flops 806027264 | bytes 6291968 | tf_op jit(solution)/shard_map/...t,ut->...u/dot_general | solution.py:41
  165.5 4.4 %fusion.13 = f32[8,4,256,256]{3,2,1,0:T(8,128)S(1)} fusion(f32[8,4,128,256]{2,3,1,0:T(8,128)S(1)} %fusion.2, s32[128]{0:T(128)S(1)} %iota_multiply_fusion), kind=kOutput, calls=%fused_computation.44 | convolution fusion | flops 1611333632 | bytes 12583424 | tf_op jit(solution)/shard_map/qp,...pu->...qu/dot_general | solution.py:42
  182.6 9.6 %all-to-all-done.6 = f32[1,4,256,256]{3,1,0,2:T(4,128)S(1)} async-done(((f32[1,4,256,256]{3,1,0,2:T(4,128)}), f32[1,4,256,256]{3,1,0,2:T(4,128)S(1)}, u32[]{:S(2)}, u32[]{:S(2)}) %all-to-all-start.6) | async-done | bytes 1048608 | tf_op jit(solution)/shard_map/all_to_all | solution.py:234
  198.1 5.9 %collective-permute-done.9.rest_9_ = f32[4,4,64,256]{3,2,1,0:T(8,128)} collective-permute-done((f32[4,4,64,256]{3,2,1,0:T(8,128)}, f32[4,4,64,256]{3,2,1,0:T(8,128)}, u32[]{:S(2)}, u32[]{:S(2)}) %collective-permute-start.9) | collective-permute-done | bytes 1048608 | tf_op jit(solution)/shard_map/ppermute | solution.py:26
  208.1 6.0 %collective-permute-start.12 = (f32[4,4,64,256]{3,2,1,0:T(8,128)S(1)}, f32[4,4,64,256]{3,2,1,0:T(8,128)}, u32[]{:S(2)}, u32[]{:S(2)}) collective-permute-start(f32[4,4,64,256]{3,2,1,0:T(8,128)S(1)} %bitcast.232), channel_id=1, source_target_pairs={{0,4},{4,8},{8,12},{12,16},{16,20},{20,24},{24,28},{1,5},{5,9},{9,... | collective-permute-start | bytes 3145736 | tf_op jit(solution)/shard_map/ppermute | solution.py:26
  214.1 4.4 %fusion = f32[8,4,128,256]{2,3,1,0:T(8,128)S(1)} fusion(f32[1,8,4,128,128]{4,3,2,1,0:T(8,128)} %bitcast.214, s32[128]{0:T(128)S(1)} %iota_multiply_fusion), kind=kOutput, calls=%fused_computation.20 | convolution fusion | flops 806027264 | bytes 6291968 | tf_op jit(solution)/shard_map/...t,ut->...u/dot_general | solution.py:41
  218.5 4.4 %fusion.10 = f32[8,4,256,256]{3,2,1,0:T(8,128)S(1)} fusion(f32[8,4,128,256]{2,3,1,0:T(8,128)S(1)} %fusion, s32[128]{0:T(128)S(1)} %iota_multiply_fusion), kind=kOutput, calls=%fused_computation.41 | convolution fusion | flops 1611333632 | bytes 12583424 | tf_op jit(solution)/shard_map/qp,...pu->...qu/dot_general | solution.py:42
  236.1 4.4 %sort.17 = (s32[768]{0:T(1024)}, s32[768]{0:T(1024)}) sort(s32[768]{0:T(1024)S(1)} %get-tuple-element.58, s32[768]{0:T(1024)S(1)} %iota.54), dimensions={0}, to_apply=%region_1.2 | sort | flops 7680 | bytes 12288 | tf_op jit(solution)/shard_map/jit(argsort)/sort | solution.py:240
  246.4 5.6 %collective-permute-done.10.rest_11_ = f32[4,4,64,256]{3,2,1,0:T(8,128)} collective-permute-done((f32[4,4,64,256]{3,2,1,0:T(8,128)S(1)}, f32[4,4,64,256]{3,2,1,0:T(8,128)}, u32[]{:S(2)}, u32[]{:S(2)}) %collective-permute-start.10) | collective-permute-done | bytes 1048608 | tf_op jit(solution)/shard_map/ppermute | solution.py:26
  254.2 6.6 %collective-permute-start.16 = (f32[4,4,64,256]{3,2,1,0:T(8,128)}, f32[4,4,64,256]{3,2,1,0:T(8,128)}, u32[]{:S(2)}, u32[]{:S(2)}) collective-permute-start(f32[4,4,64,256]{3,2,1,0:T(8,128)} %bitcast.206.rest_15_), channel_id=1, source_target_pairs={{0,4},{4,8},{8,12},{12,16},{16,20},{20,24},{24,28},{1,5},{5,9},{9,... | collective-permute-start | bytes 3145736 | tf_op jit(solution)/shard_map/ppermute | solution.py:26
  265.1 21.3 %shard_map.95 = (f32[16,4,64,256]{3,2,1,0:T(8,128)}, f32[16,4,64,256]{3,2,1,0:T(8,128)}) custom-call(s32[768]{0:T(1024)} %pad_add_fusion.1.tgt_ref, s32[768]{0:T(1024)} %get-tuple-element.65.src_ref, s32[768]{0:T(1024)} %pad_add_fusion.3.cls_ref, s32[768]{0:T(1024)} %get-tuple-element.28.order_ref, s32[2]{0:T(128)} %pad_add_fusion.4.span_ref, ...), custom_call_target="tpu_custom_call" | custom-call | flops 1610612736 | bytes 96206848 | tf_op jit(solution)/shard_map/pallas_call | solution.py:145
  286.4 8.5 %collective-permute-done.14.rest_0_ = f32[4,4,64,256]{3,2,1,0:T(8,128)} collective-permute-done((f32[4,4,64,256]{3,2,1,0:T(8,128)}, f32[4,4,64,256]{3,2,1,0:T(8,128)}, u32[]{:S(2)}, u32[]{:S(2)}) %collective-permute-start.14) | collective-permute-done | bytes 1048608 | tf_op jit(solution)/shard_map/ppermute | solution.py:26
  298.1 5.9 %collective-permute-done.17.rest_3_ = f32[4,4,64,256]{3,2,1,0:T(8,128)} collective-permute-done((f32[4,4,64,256]{3,2,1,0:T(8,128)}, f32[4,4,64,256]{3,2,1,0:T(8,128)}, u32[]{:S(2)}, u32[]{:S(2)}) %collective-permute-start.17) | collective-permute-done | bytes 1048608 | tf_op jit(solution)/shard_map/ppermute | solution.py:26
  304.0 13.6 %shard_map.96 = f32[16,4,64,256]{3,2,1,0:T(8,128)} custom-call(s32[768]{0:T(1024)} %pad_add_fusion.1.tgt_ref, s32[768]{0:T(1024)} %get-tuple-element.65.src_ref, s32[768]{0:T(1024)} %pad_add_fusion.3.cls_ref, s32[768]{0:T(1024)} %get-tuple-element.28.order_ref, s32[2]{0:T(128)} %pad_add_fusion.5.span_ref, ...), custom_call_target="tpu_custom_call", output_to_operand_aliasing={{}: (10, {})} | custom-call | flops 1610612736 | bytes 45875200 | tf_op jit(solution)/shard_map/pallas_call | solution.py:145
  (125 shorter events, 109.6 us)
Async XLA Ops:
  1.7 10.5 %copy-start.11 = (s32[192]{0:T(256)S(1)}, s32[192]{0:T(256)}, u32[]{:S(2)}) copy-start(s32[192]{0:T(256)} %param.13) | copy-start | bytes 2308
  1.7 10.5 %copy-start.12 = (s32[192]{0:T(256)S(1)}, s32[192]{0:T(256)}, u32[]{:S(2)}) copy-start(s32[192]{0:T(256)} %param.12) | copy-start | bytes 2308
  1.7 10.5 %copy-start.13 = (s32[192]{0:T(256)S(1)}, s32[192]{0:T(256)}, u32[]{:S(2)}) copy-start(s32[192]{0:T(256)} %param.14) | copy-start | bytes 2308
  1.7 16.1 %copy-start.8 = (f32[8,256,256]{2,1,0:T(8,128)S(1)}, f32[8,256,256]{2,1,0:T(8,128)}, u32[]{:S(2)}) copy-start(f32[8,256,256]{2,1,0:T(8,128)} %param.10) | copy-start | bytes 6291460
  7.3 29.1 %all-to-all-start = ((f32[4,8,4,32,128]{4,3,2,1,0:T(8,128)}), f32[4,8,4,32,128]{4,3,2,1,0:T(8,128)}, u32[]{:S(2)}, u32[]{:S(2)}) async-start(f32[4,8,4,32,128]{4,3,2,1,0:T(8,128)} %bitcast.6), calls=%async_computation | async-start | bytes 4194304 | tf_op jit(solution)/shard_map/all_to_all | solution.py:221
  12.3 32.5 %collective-permute-start = (s32[4,192]{1,0:T(4,128)S(1)}, s32[4,192]{1,0:T(4,128)S(1)}, u32[]{:S(2)}, u32[]{:S(2)}) collective-permute-start(s32[4,192]{1,0:T(4,128)S(1)} %pad_add_fusion), channel_id=1, source_target_pairs={{0,4},{4,8},{8,12},{12,16},{16,20},{20,24},{24,28},{1,5},{5,9},{9,... | collective-permute-start | bytes 9224 | tf_op jit(solution)/shard_map/ppermute | solution.py:26
  15.7 29.1 %collective-permute-start.1 = (s32[4,192]{1,0:T(4,128)S(1)}, s32[4,192]{1,0:T(4,128)S(1)}, u32[]{:S(2)}, u32[]{:S(2)}) collective-permute-start(s32[4,192]{1,0:T(4,128)S(1)} %pad_add_fusion), channel_id=1, source_target_pairs={{0,8},{4,12},{8,16},{12,20},{16,24},{20,28},{1,9},{5,13},{9,17},{1... | collective-permute-start | bytes 9224 | tf_op jit(solution)/shard_map/ppermute | solution.py:26
  36.4 30.7 %all-to-all-start.2 = ((f32[4,8,4,32,128]{4,3,2,1,0:T(8,128)}), f32[4,8,4,32,128]{4,3,2,1,0:T(8,128)}, u32[]{:S(2)}, u32[]{:S(2)}) async-start(f32[4,8,4,32,128]{4,3,2,1,0:T(8,128)} %bitcast.224), calls=%async_computation.2 | async-start | bytes 4194304 | tf_op jit(solution)/shard_map/all_to_all | solution.py:221
  67.1 18.0 %all-to-all-start.1 = ((f32[1,4,256,256]{3,1,0,2:T(4,128)}), f32[1,4,256,256]{3,1,0,2:T(4,128)S(1)}, u32[]{:S(2)}, u32[]{:S(2)}) async-start(f32[1,4,256,256]{3,1,0,2:T(4,128)} %copy.97), calls=%async_computation.1 | async-start | bytes 2097152 | tf_op jit(solution)/shard_map/all_to_all | solution.py:234
  85.1 36.6 %all-to-all-start.3 = ((f32[4,8,4,32,128]{4,3,2,1,0:T(8,128)}), f32[4,8,4,32,128]{4,3,2,1,0:T(8,128)}, u32[]{:S(2)}, u32[]{:S(2)}) async-start(f32[4,8,4,32,128]{4,3,2,1,0:T(8,128)} %bitcast.223), calls=%async_computation.3 | async-start | bytes 4194304 | tf_op jit(solution)/shard_map/all_to_all | solution.py:221
  92.5 21.0 %copy-start.4 = (f32[1,4,4,64,256]{4,3,1,2,0:T(8,128)}, f32[1,4,4,64,256]{4,3,1,2,0:T(8,128)S(1)}, u32[]{:S(2)}) copy-start(f32[1,4,4,64,256]{4,3,1,2,0:T(8,128)S(1)} %copy.155) | copy-start | bytes 3145732
  92.6 54.7 %collective-permute-start.2 = (f32[4,4,64,256]{3,2,1,0:T(8,128)S(1)}, f32[4,4,64,256]{3,2,1,0:T(8,128)}, u32[]{:S(2)}, u32[]{:S(2)}) collective-permute-start(f32[4,4,64,256]{3,2,1,0:T(8,128)S(1)} %bitcast.225), channel_id=1, source_target_pairs={{4,0},{8,4},{12,8},{16,12},{20,16},{24,20},{28,24},{5,1},{9,5},{13... | collective-permute-start | bytes 3145736 | tf_op jit(solution)/shard_map/ppermute | solution.py:26
  95.0 52.3 %collective-permute-start.3 = (f32[4,4,64,256]{3,2,1,0:T(8,128)S(1)}, f32[4,4,64,256]{3,2,1,0:T(8,128)}, u32[]{:S(2)}, u32[]{:S(2)}) collective-permute-start(f32[4,4,64,256]{3,2,1,0:T(8,128)S(1)} %bitcast.226), channel_id=1, source_target_pairs={{8,0},{12,4},{16,8},{20,12},{24,16},{28,20},{9,1},{13,5},{17,9},{2... | collective-permute-start | bytes 3145736 | tf_op jit(solution)/shard_map/ppermute | solution.py:26
  97.3 50.0 %collective-permute-start.4 = (f32[4,4,64,256]{3,2,1,0:T(8,128)S(1)}, f32[4,4,64,256]{3,2,1,0:T(8,128)}, u32[]{:S(2)}, u32[]{:S(2)}) collective-permute-start(f32[4,4,64,256]{3,2,1,0:T(8,128)S(1)} %bitcast.227), channel_id=1, source_target_pairs={{0,4},{4,8},{8,12},{12,16},{16,20},{20,24},{24,28},{1,5},{5,9},{9,... | collective-permute-start | bytes 3145736 | tf_op jit(solution)/shard_map/ppermute | solution.py:26
  102.6 44.7 %collective-permute-start.5 = (f32[4,4,64,256]{3,2,1,0:T(8,128)S(1)}, f32[4,4,64,256]{3,2,1,0:T(8,128)}, u32[]{:S(2)}, u32[]{:S(2)}) collective-permute-start(f32[4,4,64,256]{3,2,1,0:T(8,128)S(1)} %bitcast.228), channel_id=1, source_target_pairs={{0,8},{4,12},{8,16},{12,20},{16,24},{20,28},{1,9},{5,13},{9,17},{1... | collective-permute-start | bytes 3145736 | tf_op jit(solution)/shard_map/ppermute | solution.py:26
  121.7 17.2 %all-to-all-start.4 = ((f32[1,4,256,256]{3,1,0,2:T(4,128)}), f32[1,4,256,256]{3,1,0,2:T(4,128)}, u32[]{:S(2)}, u32[]{:S(2)}) async-start(f32[1,4,256,256]{3,1,0,2:T(4,128)} %copy.108), calls=%async_computation.4 | async-start | bytes 2097152 | tf_op jit(solution)/shard_map/all_to_all | solution.py:234
  138.8 37.0 %all-to-all-start.5 = ((f32[4,8,4,32,128]{4,3,2,1,0:T(8,128)}), f32[4,8,4,32,128]{4,3,2,1,0:T(8,128)}, u32[]{:S(2)}, u32[]{:S(2)}) async-start(f32[4,8,4,32,128]{4,3,2,1,0:T(8,128)} %bitcast.222), calls=%async_computation.5 | async-start | bytes 4194304 | tf_op jit(solution)/shard_map/all_to_all | solution.py:221
  147.4 48.5 %collective-permute-start.6 = (f32[4,4,64,256]{3,2,1,0:T(8,128)}, f32[4,4,64,256]{3,2,1,0:T(8,128)}, u32[]{:S(2)}, u32[]{:S(2)}) collective-permute-start(f32[4,4,64,256]{3,2,1,0:T(8,128)} %bitcast.208.rest_5_), channel_id=1, source_target_pairs={{4,0},{8,4},{12,8},{16,12},{20,16},{24,20},{28,24},{5,1},{9,5},{13... | collective-permute-start | bytes 3145736 | tf_op jit(solution)/shard_map/ppermute | solution.py:26
  150.4 45.5 %collective-permute-start.7 = (f32[4,4,64,256]{3,2,1,0:T(8,128)}, f32[4,4,64,256]{3,2,1,0:T(8,128)}, u32[]{:S(2)}, u32[]{:S(2)}) collective-permute-start(f32[4,4,64,256]{3,2,1,0:T(8,128)} %bitcast.208.rest_5_), channel_id=1, source_target_pairs={{8,0},{12,4},{16,8},{20,12},{24,16},{28,20},{9,1},{13,5},{17,9},{2... | collective-permute-start | bytes 3145736 | tf_op jit(solution)/shard_map/ppermute | solution.py:26
  153.2 44.9 %collective-permute-start.8 = (f32[4,4,64,256]{3,2,1,0:T(8,128)}, f32[4,4,64,256]{3,2,1,0:T(8,128)}, u32[]{:S(2)}, u32[]{:S(2)}) collective-permute-start(f32[4,4,64,256]{3,2,1,0:T(8,128)} %bitcast.208.rest_5_), channel_id=1, source_target_pairs={{0,4},{4,8},{8,12},{12,16},{16,20},{20,24},{24,28},{1,5},{5,9},{9,... | collective-permute-start | bytes 3145736 | tf_op jit(solution)/shard_map/ppermute | solution.py:26
  159.0 45.0 %collective-permute-start.9 = (f32[4,4,64,256]{3,2,1,0:T(8,128)}, f32[4,4,64,256]{3,2,1,0:T(8,128)}, u32[]{:S(2)}, u32[]{:S(2)}) collective-permute-start(f32[4,4,64,256]{3,2,1,0:T(8,128)} %bitcast.208.rest_5_), channel_id=1, source_target_pairs={{0,8},{4,12},{8,16},{12,20},{16,24},{20,28},{1,9},{5,13},{9,17},{1... | collective-permute-start | bytes 3145736 | tf_op jit(solution)/shard_map/ppermute | solution.py:26
  175.9 16.3 %all-to-all-start.6 = ((f32[1,4,256,256]{3,1,0,2:T(4,128)}), f32[1,4,256,256]{3,1,0,2:T(4,128)S(1)}, u32[]{:S(2)}, u32[]{:S(2)}) async-start(f32[1,4,256,256]{3,1,0,2:T(4,128)} %copy.117), calls=%async_computation.6 | async-start | bytes 2097152 | tf_op jit(solution)/shard_map/all_to_all | solution.py:234
  194.6 37.3 %copy-start.5 = (f32[1,4,4,64,256]{4,3,1,2,0:T(8,128)}, f32[1,4,4,64,256]{4,3,1,2,0:T(8,128)S(1)}, u32[]{:S(2)}) copy-start(f32[1,4,4,64,256]{4,3,1,2,0:T(8,128)S(1)} %copy.153) | copy-start | bytes 3145732
  204.0 48.0 %collective-permute-start.10 = (f32[4,4,64,256]{3,2,1,0:T(8,128)S(1)}, f32[4,4,64,256]{3,2,1,0:T(8,128)}, u32[]{:S(2)}, u32[]{:S(2)}) collective-permute-start(f32[4,4,64,256]{3,2,1,0:T(8,128)S(1)} %bitcast.230), channel_id=1, source_target_pairs={{4,0},{8,4},{12,8},{16,12},{20,16},{24,20},{28,24},{5,1},{9,5},{13... | collective-permute-start | bytes 3145736 | tf_op jit(solution)/shard_map/ppermute | solution.py:26
  205.9 48.3 %collective-permute-start.11 = (f32[4,4,64,256]{3,2,1,0:T(8,128)S(1)}, f32[4,4,64,256]{3,2,1,0:T(8,128)}, u32[]{:S(2)}, u32[]{:S(2)}) collective-permute-start(f32[4,4,64,256]{3,2,1,0:T(8,128)S(1)} %bitcast.231), channel_id=1, source_target_pairs={{8,0},{12,4},{16,8},{20,12},{24,16},{28,20},{9,1},{13,5},{17,9},{2... | collective-permute-start | bytes 3145736 | tf_op jit(solution)/shard_map/ppermute | solution.py:26
  208.1 52.7 %collective-permute-start.12 = (f32[4,4,64,256]{3,2,1,0:T(8,128)S(1)}, f32[4,4,64,256]{3,2,1,0:T(8,128)}, u32[]{:S(2)}, u32[]{:S(2)}) collective-permute-start(f32[4,4,64,256]{3,2,1,0:T(8,128)S(1)} %bitcast.232), channel_id=1, source_target_pairs={{0,4},{4,8},{8,12},{12,16},{16,20},{20,24},{24,28},{1,5},{5,9},{9,... | collective-permute-start | bytes 3145736 | tf_op jit(solution)/shard_map/ppermute | solution.py:26
  226.6 16.6 %all-to-all-start.7 = ((f32[1,4,256,256]{3,1,0,2:T(4,128)}), f32[1,4,256,256]{3,1,0,2:T(4,128)S(1)}, u32[]{:S(2)}, u32[]{:S(2)}) async-start(f32[1,4,256,256]{3,1,0,2:T(4,128)} %copy.124), calls=%async_computation.7 | async-start | bytes 2097152 | tf_op jit(solution)/shard_map/all_to_all | solution.py:234
  231.8 32.2 %collective-permute-start.13 = (f32[4,4,64,256]{3,2,1,0:T(8,128)S(1)}, f32[4,4,64,256]{3,2,1,0:T(8,128)S(1)}, u32[]{:S(2)}, u32[]{:S(2)}) collective-permute-start(f32[4,4,64,256]{3,2,1,0:T(8,128)S(1)} %bitcast.233), channel_id=1, source_target_pairs={{0,8},{4,12},{8,16},{12,20},{16,24},{20,28},{1,9},{5,13},{9,17},{1... | collective-permute-start | bytes 3145736 | tf_op jit(solution)/shard_map/ppermute | solution.py:26
  244.4 50.5 %collective-permute-start.14 = (f32[4,4,64,256]{3,2,1,0:T(8,128)}, f32[4,4,64,256]{3,2,1,0:T(8,128)}, u32[]{:S(2)}, u32[]{:S(2)}) collective-permute-start(f32[4,4,64,256]{3,2,1,0:T(8,128)} %bitcast.206.rest_15_), channel_id=1, source_target_pairs={{4,0},{8,4},{12,8},{16,12},{20,16},{24,20},{28,24},{5,1},{9,5},{13... | collective-permute-start | bytes 3145736 | tf_op jit(solution)/shard_map/ppermute | solution.py:26
  252.0 43.0 %collective-permute-start.15 = (f32[4,4,64,256]{3,2,1,0:T(8,128)}, f32[4,4,64,256]{3,2,1,0:T(8,128)}, u32[]{:S(2)}, u32[]{:S(2)}) collective-permute-start(f32[4,4,64,256]{3,2,1,0:T(8,128)} %bitcast.206.rest_15_), channel_id=1, source_target_pairs={{8,0},{12,4},{16,8},{20,12},{24,16},{28,20},{9,1},{13,5},{17,9},{2... | collective-permute-start | bytes 3145736 | tf_op jit(solution)/shard_map/ppermute | solution.py:26
  254.2 44.0 %collective-permute-start.16 = (f32[4,4,64,256]{3,2,1,0:T(8,128)}, f32[4,4,64,256]{3,2,1,0:T(8,128)}, u32[]{:S(2)}, u32[]{:S(2)}) collective-permute-start(f32[4,4,64,256]{3,2,1,0:T(8,128)} %bitcast.206.rest_15_), channel_id=1, source_target_pairs={{0,4},{4,8},{8,12},{12,16},{16,20},{20,24},{24,28},{1,5},{5,9},{9,... | collective-permute-start | bytes 3145736 | tf_op jit(solution)/shard_map/ppermute | solution.py:26
  260.8 43.2 %collective-permute-start.17 = (f32[4,4,64,256]{3,2,1,0:T(8,128)}, f32[4,4,64,256]{3,2,1,0:T(8,128)}, u32[]{:S(2)}, u32[]{:S(2)}) collective-permute-start(f32[4,4,64,256]{3,2,1,0:T(8,128)} %bitcast.206.rest_15_), channel_id=1, source_target_pairs={{0,8},{4,12},{8,16},{12,20},{16,24},{20,28},{1,9},{5,13},{9,17},{1... | collective-permute-start | bytes 3145736 | tf_op jit(solution)/shard_map/ppermute | solution.py:26
  (8 other events, 36.3 us)
